TPU v7x, 128 devices: a whole 4x4x4 slice. The times are simulated.
128 devices in a mesh: tm: 8 (over y_hi, x), space: 16 (over y_lo, z, core).
Axes of the slice: x: 4, y: 4 (y_hi: 2, y_lo: 2; y = y_hi * 2 + y_lo), z: 4, core: 2. Of those that a mesh axis runs over, the one named last changes fastest.
Arguments:
- video: bfloat16 [2, 16, 32, 48, 384], P(None, 'tm', 'space'), may hold values from -6 to 6
- conv_weight: bfloat16 [10368, 384], replicated, may hold values from -0.0625 to 0.0625
- norm_gain: bfloat16 [384], replicated, may hold values from 0.099609375 to 1.8984375
- down_weight: bfloat16 [3456, 384], replicated, may hold values from -0.109375 to 0.109375
- clip_lengths: int32 [2], replicated, may hold values from 1 to 16, as said below
- cotangent: bfloat16 [2, 16, 16, 24, 384], P(None, 'tm', 'space'), may hold values from -6 to 6
Outputs:
- latent: bfloat16 [2, 16, 16, 24, 384], P(None, 'tm', 'space')
- grad_conv: float32 [3981312], P(('tm', 'space'))
- grad_down: float32 [1327104], P(('tm', 'space'))
Inputs may be any that keep to these rules, and one draw needn't show every extreme that they name: `clip_lengths`: clip 0 is full, with 16 valid frames.
All inputs are finite; a program needn't handle non-finite values.
Results may differ from a plain program's by a relative error of at most 0.015.
Values may be sent and summed in bfloat16 or wider, within the bound.
No kernel may reach another device: no remote copies, remote signals or barrier semaphores. Data moves between devices by JAX's collectives and lax.ppermute only.
A program may use at most 128 MiB of HBM per device.

v0:
```python
import jax
import jax.numpy as jnp
from jax import lax
from jax.sharding import PartitionSpec as P

EPSILON = 1e-06


def from_behind(array, axis, by):
    count = lax.axis_size(axis)
    pairs = [(i, i + by) for i in range(count) if 0 <= i + by < count]
    return lax.ppermute(array, axis, pairs)


def padded_2(array, sides, width):
    for axis, dim in sides:
        count, length = (lax.axis_size(axis), array.shape[dim])
        up = [(i, (i + 1) % count) for i in range(count - 1)]
        down = [(j, i) for i, j in up]
        last = lax.slice_in_dim(array, length - width, length, axis=dim)
        first = lax.slice_in_dim(array, 0, width, axis=dim)
        before = lax.ppermute(last, axis, up)
        after = lax.ppermute(first, axis, down)
        array = jnp.concatenate([before, array, after], axis=dim)
    return array


def norm_act(conv_out, norm_gain, keeper):
    scale = lax.rsqrt(jnp.mean(conv_out * conv_out, axis=-1, keepdims=True) + EPSILON)
    normed = conv_out * scale * norm_gain.astype(jnp.float32)
    return (normed * jax.nn.sigmoid(normed) * keeper).astype(jnp.bfloat16)


def norm_back(conv_out, norm_gain, keeper, upstream):
    scale = lax.rsqrt(jnp.mean(conv_out * conv_out, axis=-1, keepdims=True) + EPSILON)
    unit = conv_out * scale
    gained = norm_gain.astype(jnp.float32)
    normed = unit * gained
    sigma = jax.nn.sigmoid(normed)
    d_normed = upstream * keeper * sigma * (1.0 + normed * (1.0 - sigma))
    d_unit = d_normed * gained
    return (scale * (d_unit - unit * jnp.mean(d_unit * unit, axis=-1, keepdims=True))).astype(
        jnp.bfloat16
    )


def conv_window(padded, tap, frames, rows, start):
    width = padded.shape[3] - 2
    frame_tap = tap // 9
    row_tap = tap // 3 % 3
    col_tap = tap % 3
    return padded[
        :,
        frame_tap : frame_tap + frames,
        start + row_tap : start + row_tap + rows,
        col_tap : col_tap + width,
    ]


def causal_conv(padded, conv_weight, frames, rows, start):
    channels = padded.shape[-1]
    width = padded.shape[3] - 2
    shape = (padded.shape[0], frames, rows, width, channels)
    total = jnp.zeros(shape, jnp.float32)
    for tap in range(27):
        window = conv_window(padded, tap, frames, rows, start).reshape(-1, channels)
        block = conv_weight[tap * channels : (tap + 1) * channels]
        total = total + jnp.dot(window, block, preferred_element_type=jnp.float32).reshape(shape)
    return total


def conv_weight_grad(padded, d_conv, frames, rows, start):
    channels = padded.shape[-1]
    flat_grad = d_conv.reshape(-1, channels)
    blocks = []
    for tap in range(27):
        window = conv_window(padded, tap, frames, rows, start).reshape(-1, channels)
        blocks.append(jnp.dot(window.T, flat_grad, preferred_element_type=jnp.float32))
    return jnp.stack(blocks).reshape(-1)


def down_window(hpad, tap):
    out_rows = (hpad.shape[2] - 1) // 2
    out_cols = (hpad.shape[3] - 1) // 2
    row_tap = tap // 3
    col_tap = tap % 3
    return hpad[:, :, row_tap : row_tap + 2 * out_rows : 2, col_tap : col_tap + 2 * out_cols : 2]


def down_forward(hpad, down_weight):
    channels = hpad.shape[-1]
    shape = (
        hpad.shape[0],
        hpad.shape[1],
        (hpad.shape[2] - 1) // 2,
        (hpad.shape[3] - 1) // 2,
        channels,
    )
    total = jnp.zeros(shape, jnp.float32)
    for tap in range(9):
        window = down_window(hpad, tap).reshape(-1, channels)
        block = down_weight[tap * channels : (tap + 1) * channels]
        total = total + jnp.dot(window, block, preferred_element_type=jnp.float32).reshape(shape)
    return total


def down_weight_grad(hpad, cotangent):
    channels = hpad.shape[-1]
    flat_cot = cotangent.reshape(-1, channels)
    blocks = []
    for tap in range(9):
        window = down_window(hpad, tap).reshape(-1, channels)
        blocks.append(jnp.dot(window.T, flat_cot, preferred_element_type=jnp.float32))
    return jnp.stack(blocks).reshape(-1)


def down_back(hpad_shape, cotangent, down_weight):
    channels = cotangent.shape[-1]
    out_rows = cotangent.shape[2]
    out_cols = cotangent.shape[3]
    flat_cot = cotangent.reshape(-1, channels)
    d_pad = jnp.zeros(hpad_shape, jnp.float32)
    for tap in range(9):
        row_tap = tap // 3
        col_tap = tap % 3
        block = down_weight[tap * channels : (tap + 1) * channels]
        piece = jnp.dot(flat_cot, block.T, preferred_element_type=jnp.float32).reshape(
            cotangent.shape
        )
        d_pad = d_pad.at[
            :, :, row_tap : row_tap + 2 * out_rows : 2, col_tap : col_tap + 2 * out_cols : 2
        ].add(piece)
    return d_pad


def local(video, conv_weight, norm_gain, down_weight, clip_lengths, cotangent):
    frames = video.shape[1]
    rows = video.shape[2]
    width = video.shape[3]
    first_frame = lax.axis_index("tm") * frames
    frame_ids = first_frame + jnp.arange(frames, dtype=jnp.int32)
    keeper = (frame_ids[None, :] < clip_lengths[:, None]).astype(jnp.float32)[
        :, :, None, None, None
    ]
    masked = video * keeper.astype(jnp.bfloat16)
    earlier = from_behind(masked, "tm", 1)
    joined = jnp.concatenate([earlier, masked], axis=1)
    depth = 1
    extended = padded_2(joined, (("space", 2),), depth)
    padded = jnp.pad(extended, ((0, 0), (0, 0), (0, 0), (1, 1), (0, 0)))
    conv_out = causal_conv(padded, conv_weight, frames, rows, 0)
    hidden = norm_act(conv_out, norm_gain, keeper)
    below = from_behind(hidden[:, :, :1], "space", -1)
    hidden_rows = jnp.concatenate([hidden, below], axis=2)
    grad_start = 0
    hpad = jnp.pad(hidden_rows, ((0, 0), (0, 0), (0, 0), (0, 1), (0, 0)))
    latent = down_forward(hpad, down_weight).astype(jnp.bfloat16)
    grad_down_term = down_weight_grad(hpad, cotangent)
    d_pad = down_back(hpad.shape, cotangent, down_weight)
    carried = from_behind(
        d_pad[:, :, rows : rows + 1, :width].astype(jnp.bfloat16), "space", 1
    ).astype(jnp.float32)
    d_hidden = d_pad[:, :, :rows, :width] + jnp.pad(
        carried, ((0, 0), (0, 0), (0, rows - 1), (0, 0), (0, 0))
    )
    d_conv = norm_back(conv_out, norm_gain, keeper, d_hidden)
    grad_conv_term = conv_weight_grad(padded, d_conv, frames, rows, grad_start)
    devices = lax.axis_size("tm") * lax.axis_size("space")
    conv_share = grad_conv_term.shape[0] // devices
    combined = jnp.concatenate(
        [grad_conv_term.reshape(devices, -1), grad_down_term.reshape(devices, -1)], axis=1
    ).reshape(-1)
    reduced = lax.psum_scatter(combined, ("tm", "space"), scatter_dimension=0, tiled=True)
    return (latent, reduced[:conv_share], reduced[conv_share:])


def solution(mesh):
    in_specs = (
        P(None, "tm", "space", None, None),
        P(),
        P(),
        P(),
        P(),
        P(None, "tm", "space", None, None),
    )
    out_specs = (P(None, "tm", "space", None, None), P(("tm", "space")), P(("tm", "space")))
    return jax.shard_map(local, mesh=mesh, in_specs=in_specs, out_specs=out_specs, check_vma=False)
```

profile of v0, /device:TPU:1, one launch (start us, length us, event | category | flops | bytes accessed | tf_op | source)
XLA Modules:
  0.0 457.5 jit_solution(8844339701358337750)
XLA Ops:
  9.2 4.0 collective-permute-start
  26.9 5.0 %scatter_fusion = f32[2,2,3,49,384]{4,1,3,2,0:T(2,128)} fusion(f32[2,2,3,49,384]{4,1,3,2,0:T(2,128)} %broadcast_in_dim.2, s32[24]{0:T(128)S(1)} %get-tuple-element.39, f32[24,2,2,384]{3,2,1,0:T(2,128)} %copy.69), kind=kCustom, calls=%fused_computation | custom fusion | flops 36864 | bytes 442560 | tf_op jit(solution)/shard_map/scatter-add | solution.py:132
  32.0 5.1 %scatter_fusion.1 = f32[2,2,3,49,384]{4,1,3,2,0:T(2,128)} fusion(f32[2,2,3,49,384]{4,1,3,2,0:T(2,128)} %scatter_fusion, s32[24]{0:T(128)S(1)} %get-tuple-element.41, f32[24,2,2,384]{3,2,1,0:T(2,128)} %copy.70), kind=kCustom, calls=%fused_computation.1 | custom fusion | flops 36864 | bytes 442560 | tf_op jit(solution)/shard_map/scatter-add | solution.py:132
  37.0 5.1 %scatter_fusion.2 = f32[2,2,3,49,384]{4,1,3,2,0:T(2,128)} fusion(f32[2,2,3,49,384]{4,1,3,2,0:T(2,128)} %scatter_fusion.1, s32[24]{0:T(128)S(1)} %get-tuple-element.43, f32[24,2,2,384]{3,2,1,0:T(2,128)} %copy.71), kind=kCustom, calls=%fused_computation.2 | custom fusion | flops 36864 | bytes 442560 | tf_op jit(solution)/shard_map/scatter-add | solution.py:132
  42.1 5.0 %scatter_fusion.3 = f32[2,2,3,49,384]{4,1,3,2,0:T(2,128)} fusion(f32[2,2,3,49,384]{4,1,3,2,0:T(2,128)} %scatter_fusion.2, s32[24]{0:T(128)S(1)} %get-tuple-element.40, f32[24,2,2,384]{3,2,1,0:T(2,128)} %copy.72), kind=kCustom, calls=%fused_computation.3 | custom fusion | flops 36864 | bytes 442560 | tf_op jit(solution)/shard_map/scatter-add | solution.py:132
  47.1 5.1 %scatter_fusion.4 = f32[2,2,3,49,384]{4,1,3,2,0:T(2,128)} fusion(f32[2,2,3,49,384]{4,1,3,2,0:T(2,128)} %scatter_fusion.3, s32[24]{0:T(128)S(1)} %get-tuple-element.42, f32[24,2,2,384]{3,2,1,0:T(2,128)} %copy.73), kind=kCustom, calls=%fused_computation.4 | custom fusion | flops 36864 | bytes 442560 | tf_op jit(solution)/shard_map/scatter-add | solution.py:132
  52.2 5.0 %scatter_fusion.5 = f32[2,2,3,49,384]{4,1,3,2,0:T(2,128)} fusion(f32[2,2,3,49,384]{4,1,3,2,0:T(2,128)} %scatter_fusion.4, s32[24]{0:T(128)S(1)} %get-tuple-element.44, f32[24,2,2,384]{3,2,1,0:T(2,128)} %copy.74), kind=kCustom, calls=%fused_computation.5 | custom fusion | flops 36864 | bytes 442560 | tf_op jit(solution)/shard_map/scatter-add | solution.py:132
  57.2 5.3 %scatter_fusion.6 = f32[2,2,3,49,384]{4,1,3,2,0:T(2,128)} fusion(f32[2,2,3,49,384]{4,1,3,2,0:T(2,128)} %scatter_fusion.5, s32[24]{0:T(128)S(1)} %fusion.256, f32[24,2,2,384]{3,2,1,0:T(2,128)} %copy.75), kind=kCustom, calls=%fused_computation.6 | custom fusion | flops 36864 | bytes 442560 | tf_op jit(solution)/shard_map/scatter-add | solution.py:132
  62.5 5.3 %scatter_fusion.7 = f32[2,2,3,49,384]{4,1,3,2,0:T(2,128)} fusion(f32[2,2,3,49,384]{4,1,3,2,0:T(2,128)} %scatter_fusion.6, s32[24]{0:T(128)S(1)} %fusion.257, f32[24,2,2,384]{3,2,1,0:T(2,128)} %copy.76), kind=kCustom, calls=%fused_computation.7 | custom fusion | flops 36864 | bytes 442560 | tf_op jit(solution)/shard_map/scatter-add | solution.py:132
  67.8 5.0 %scatter_fusion.8 = f32[2,2,3,49,384]{4,1,3,2,0:T(2,128)} fusion(f32[2,2,3,49,384]{4,1,3,2,0:T(2,128)} %scatter_fusion.7, s32[24]{0:T(128)S(1)} %fusion.258, f32[24,2,2,384]{3,2,1,0:T(2,128)S(1)} %copy.77), kind=kCustom, calls=%fused_computation.8 | custom fusion | flops 36864 | bytes 442560 | tf_op jit(solution)/shard_map/scatter-add | solution.py:132
  73.9 4.4 collective-permute-start.4
  78.3 1.4 fusion.60
  79.9 1.9 collective-permute-start.2
  81.8 3.8 collective-permute-start.1
  85.6 1.3 fusion.49
  86.9 1.3 fusion.95
  89.7 1.3 fusion.52
  91.0 1.3 fusion.56
  92.3 1.3 fusion.58
  93.6 1.3 fusion.62
  96.2 1.3 fusion.68
  104.8 8.3 %multiply_reduce_fusion.1 = (f32[2,2,2,48]{1,3,2,0:T(8,128)S(1)}, f32[2,2,2,48,384]{4,1,3,2,0:T(2,128)S(1)}) fusion(f32[2,2,2,48,384]{4,3,2,1,0:T(8,128)S(1)} %fusion.52, f32[2,2,2,48,384]{4,3,2,1,0:T(8,128)S(1)} %fusion.54, f32[2,2,2,48,384]{4,3,2,1,0:T(8,128)S(1)} %fusion.56, f32[2,2,2,48,384]{4,3,2,1,0:T(8,128)S(1)} %fusion.58, ...), kind=kLoop, calls=%fused_computation.153 | loop fusion | flops 3833472 | bytes 15336960 | tf_op jit(solution)/shard_map/reduce_sum | solution.py:29
  113.1 2.0 multiply_reduce_fusion
  116.0 1.9 collective-permute-start.3
  150.8 14.7 %reshape_reshape.6 = f32[128,31104]{1,0:T(8,128)} reshape(f32[27,384,384]{2,1,0:T(8,128)} %fusion.19) | data formatting | bytes 31850496 | tf_op jit(solution)/shard_map/reshape;reshape | solution.py:171
  165.5 1.3 fusion.48
  177.1 5.8 %reshape_reshape.7 = f32[128,10368]{1,0:T(8,128)} reshape(f32[9,384,384]{2,1,0:T(8,128)} %fusion.10) | data formatting | bytes 10616832 | tf_op jit(solution)/shard_map/reshape;reshape | solution.py:171
  182.9 16.3 %pad_maximum_fusion = f32[128,41472]{1,0:T(8,128)} fusion(f32[128,10368]{1,0:T(8,128)} %reshape_reshape.7, f32[128,31104]{1,0:T(8,128)} %reshape_reshape.6), kind=kLoop, calls=%fused_computation.9 | loop fusion | flops 5308416 | bytes 42467328 | tf_op jit(solution)/shard_map/concatenate | solution.py:170
  199.2 20.0 %reshape.364 = f32[5308416]{0:T(1024)} reshape(f32[128,41472]{1,0:T(8,128)} %pad_maximum_fusion) | data formatting | bytes 42467328 | tf_op jit(solution)/shard_map/reshape | solution.py:172
  221.8 225.7 %all-reduce.15.cloned.1.call-done = f32[5308416]{0:T(1024)} async-done(((f32[5308416]{0:T(1024)}), f32[5308416]{0:T(1024)}) %all-reduce.15.cloned.1.call-update) | async-done | bytes 21233680
  447.5 1.7 dynamic-slice.1
  449.1 1.5 dynamic-slice.2
  (132 shorter events, 73.0 us)
Async XLA Ops:
  7.2 6.0 %copy-start = (bf16[2,2,1,24,384]{4,3,2,1,0:T(8,128)(2,1)S(1)}, bf16[2,2,1,24,384]{4,3,2,1,0:T(8,128)(2,1)}, u32[]{:S(2)}) copy-start(bf16[2,2,1,24,384]{4,3,2,1,0:T(8,128)(2,1)} %param.11) | copy-start | bytes 221188
  7.2 11.0 %copy-start.1 = (bf16[3456,384]{1,0:T(8,128)(2,1)S(1)}, bf16[3456,384]{1,0:T(8,128)(2,1)}, u32[]{:S(2)}) copy-start(bf16[3456,384]{1,0:T(8,128)(2,1)} %param.9) | copy-start | bytes 7962628
  7.2 440.3 %all-reduce.15.cloned.1.call-start = ((), (), s32[]{:S(2)}) async-start(), calls=%async_computation | async-start | bytes 42467328
  9.2 70.6 %collective-permute-start = (bf16[2,2,2,48,384]{4,3,2,1,0:T(8,128)(2,1)S(1)}, bf16[2,2,2,48,384]{4,3,2,1,0:T(8,128)(2,1)S(1)}, u32[]{:S(2)}, u32[]{:S(2)}) collective-permute-start(bf16[2,2,2,48,384]{4,3,2,1,0:T(8,128)(2,1)S(1)} %broadcast_multiply_fusion.1), channel_id=1, source_target_pairs={{0,16},{16,32},{32,48},{48,64},{64,80},{80,96},{96,112},{1,17},{17... | collective-permute-start | bytes 884744 | tf_op jit(solution)/shard_map/ppermute | solution.py:12
  25.8 52.5 %copy-start.5 = (bf16[384]{0:T(512)(128)(2,1)S(1)}, bf16[384]{0:T(512)(128)(2,1)}, u32[]{:S(2)}) copy-start(bf16[384]{0:T(512)(128)(2,1)} %param.8) | copy-start | bytes 2308
  73.9 39.2 %collective-permute-start.4 = (bf16[2,2,1,48,384]{4,1,3,2,0:T(2,128)(2,1)S(1)}, bf16[2,2,1,48,384]{4,1,3,2,0:T(2,128)(2,1)S(1)}, u32[]{:S(2)}, u32[]{:S(2)}) collective-permute-start(bf16[2,2,1,48,384]{4,1,3,2,0:T(2,128)(2,1)S(1)} %slice.763), channel_id=1, source_target_pairs={{0,1},{1,2},{2,3},{3,4},{4,5},{5,6},{6,7},{7,8},{8,9},{9,10},{10,1... | collective-permute-start | bytes 442376 | tf_op jit(solution)/shard_map/ppermute | solution.py:12
  78.3 19.2 %slice-start = ((s8[7962624]{0:T(1024)(128)(4,1)}), s8[4194304]{0:T(1024)(128)(4,1)S(1)}, s32[]{:S(2)}) async-start(s8[7962624]{0:T(1024)(128)(4,1)} %bitcast.603), calls=%async_computation.1 | async-start | bytes 8388608
  79.9 8.4 %collective-permute-start.2 = (bf16[2,4,1,48,384]{4,3,2,1,0:T(8,128)(2,1)S(1)}, bf16[2,4,1,48,384]{4,3,2,1,0:T(8,128)(2,1)S(1)}, u32[]{:S(2)}, u32[]{:S(2)}) collective-permute-start(bf16[2,4,1,48,384]{4,3,2,1,0:T(8,128)(2,1)S(1)} %get-tuple-element.18), channel_id=1, source_target_pairs={{1,0},{2,1},{3,2},{4,3},{5,4},{6,5},{7,6},{8,7},{9,8},{10,9},{11,1... | collective-permute-start | bytes 884744 | tf_op jit(solution)/shard_map/ppermute | solution.py:23
  81.8 7.3 %collective-permute-start.1 = (bf16[2,4,1,48,384]{4,3,2,1,0:T(8,128)(2,1)S(1)}, bf16[2,4,1,48,384]{4,3,2,1,0:T(8,128)(2,1)S(1)}, u32[]{:S(2)}, u32[]{:S(2)}) collective-permute-start(bf16[2,4,1,48,384]{4,3,2,1,0:T(8,128)(2,1)S(1)} %get-tuple-element.17), channel_id=1, source_target_pairs={{0,1},{1,2},{2,3},{3,4},{4,5},{5,6},{6,7},{7,8},{8,9},{9,10},{10,1... | collective-permute-start | bytes 884744 | tf_op jit(solution)/shard_map/ppermute | solution.py:22
  88.2 9.3 %slice-start.1 = ((s8[7962624]{0:T(1024)(128)(4,1)}), s8[3768320]{0:T(1024)(128)(4,1)S(1)}, s32[]{:S(2)}) async-start(s8[7962624]{0:T(1024)(128)(4,1)} %bitcast.603), calls=%async_computation.2 | async-start | bytes 7536640
  104.8 8.4 %copy-start.2 = (f32[2,2,3,49,384]{4,1,3,2,0:T(2,128)S(1)}, f32[2,2,3,49,384]{4,1,3,2,0:T(2,128)}, u32[]{:S(2)}) copy-start(f32[2,2,3,49,384]{4,1,3,2,0:T(2,128)} %scatter_fusion.8) | copy-start | bytes 2709508
  115.1 0.7 copy-start.3
  116.0 49.6 %collective-permute-start.3 = (bf16[2,2,1,48,384]{4,1,3,2,0:T(2,128)(2,1)S(1)}, bf16[2,2,1,48,384]{4,1,3,2,0:T(2,128)(2,1)}, u32[]{:S(2)}, u32[]{:S(2)}) collective-permute-start(bf16[2,2,1,48,384]{4,1,3,2,0:T(2,128)(2,1)S(1)} %slice.423), channel_id=1, source_target_pairs={{1,0},{2,1},{3,2},{4,3},{5,4},{6,5},{7,6},{8,7},{9,8},{10,9},{11,1... | collective-permute-start | bytes 442376 | tf_op jit(solution)/shard_map/ppermute | solution.py:12
  150.8 14.7 %copy-start.4 = (bf16[2,2,2,48,384]{4,1,3,2,0:T(2,128)(2,1)S(1)}, bf16[2,2,2,48,384]{4,1,3,2,0:T(2,128)(2,1)}, u32[]{:S(2)}) copy-start(bf16[2,2,2,48,384]{4,1,3,2,0:T(2,128)(2,1)} %copy-done.3) | copy-start | bytes 884740
Sparse Core Ops, SparseCore 0:
  219.4 228.0 all-reduce.14
where the time goes:
time: 460 us; the launch traced here: 457 us
  waiting for transfers between devices  227 us (49%)
  other arithmetic  78.2 us (17%)
  matrix products  68.8 us (15%)
  local copies, waits for them, and re-layouts  53.2 us (12%)
  starting transfers between devices  16 us (3%)
  between operations  14.7 us (3%)
    unnamed x2, waiting for transfers between devices  226 us
    scatter-add x9, other arithmetic, down_back(): d_pad = d_pad.at[:, :, row_tap:row_tap + 2 * out_rows:2, col_tap:col_tap...  45.9 us
    dot_general x27, matrix products, conv_weight_grad(): jnp.dot(window.T, flat_grad, preferred_element_type=jnp.float32)  32.3 us
    reshape x1, local copies, waits for them, and re-layouts, local(): combined = jnp.concatenate([grad_conv_term.reshape(devices, -1), grad_dow...  20 us
    dot_general x27, matrix products, causal_conv(): jnp.dot(window, block, preferred_element_type=jnp.float32).reshape(shape)  17.8 us
    concatenate x1, other arithmetic, local(): jnp.concatenate([grad_conv_term.reshape(devices, -1), grad_down_term.resh...  16.3 us
    another operation x1, local copies, waits for them, and re-layouts, local(): grad_conv_term.reshape(devices, -1)  14.7 us
    ppermute x3, starting transfers between devices, from_behind(): return lax.ppermute(array, axis, pairs)  10.3 us
  transfers between devices with their start and end apart: 6, of which 2 were waited for; matrix products, arithmetic and copies ran while one was open for 30% of the time, Pallas kernels for 0%

commit v1 on v0

v1 whole, which is shorter than its diff:
```python
import jax
import jax.numpy as jnp
from jax import lax
from jax.sharding import PartitionSpec as P

EPSILON = 1e-06


def shifted(array, axes, moves):
    sizes = [lax.axis_size(a) for a in axes]
    total = 1
    for n in sizes:
        total *= n
    pairs = []
    for src in range(total):
        coords, rest = [], src
        for n in reversed(sizes):
            coords.append(rest % n)
            rest //= n
        coords = coords[::-1]
        dst = [c + m for c, m in zip(coords, moves)]
        if all(0 <= d < n for d, n in zip(dst, sizes)):
            flat = 0
            for d, n in zip(dst, sizes):
                flat = flat * n + d
            pairs.append((src, flat))
    name = axes[0] if len(axes) == 1 else tuple(axes)
    return lax.ppermute(array, name, pairs)


def norm_act(conv_out, norm_gain, keeper):
    scale = lax.rsqrt(jnp.mean(conv_out * conv_out, axis=-1, keepdims=True) + EPSILON)
    normed = conv_out * scale * norm_gain.astype(jnp.float32)
    return (normed * jax.nn.sigmoid(normed) * keeper).astype(jnp.bfloat16)


def norm_back(conv_out, norm_gain, keeper, upstream):
    scale = lax.rsqrt(jnp.mean(conv_out * conv_out, axis=-1, keepdims=True) + EPSILON)
    unit = conv_out * scale
    gained = norm_gain.astype(jnp.float32)
    normed = unit * gained
    sigma = jax.nn.sigmoid(normed)
    d_normed = upstream * keeper * sigma * (1.0 + normed * (1.0 - sigma))
    d_unit = d_normed * gained
    return (scale * (d_unit - unit * jnp.mean(d_unit * unit, axis=-1, keepdims=True))).astype(
        jnp.bfloat16
    )


def local(video, conv_weight, norm_gain, down_weight, clip_lengths, cotangent):
    clips, frames, rows, width, channels = video.shape
    t = lax.axis_index("tm")
    s = lax.axis_index("space")
    last = lax.axis_size("space") - 1
    frame_ids = t * frames + jnp.arange(frames, dtype=jnp.int32)
    keeper = (frame_ids[None, :] < clip_lengths[:, None]).astype(jnp.float32)[
        :, :, None, None, None
    ]
    masked = video * keeper.astype(jnp.bfloat16)

    top = masked[:, :, rows - 1 :]
    above = shifted(top, ("space",), (1,))
    below = shifted(masked, ("space",), (-1,))
    prev = shifted(masked, ("tm",), (1,))
    prev_above = shifted(top, ("tm", "space"), (1, 1))
    prev_below = shifted(masked, ("tm", "space"), (1, -1))
    cot_above = shifted(cotangent, ("space",), (1,))

    own = jnp.concatenate([above, masked, below], axis=2)
    old = jnp.concatenate([prev_above, prev, prev_below], axis=2)
    padded = jnp.pad(
        jnp.concatenate([old, own], axis=1), ((0, 0), (0, 0), (0, 0), (1, 1), (0, 0))
    )

    kernel3 = conv_weight.reshape(3, 3, 3, channels, channels)
    conv_out = lax.conv_general_dilated(
        padded,
        kernel3,
        window_strides=(1, 1, 1),
        padding="VALID",
        dimension_numbers=("NDHWC", "DHWIO", "NDHWC"),
        preferred_element_type=jnp.float32,
    )
    hidden = norm_act(conv_out, norm_gain, keeper)
    row_ids = jnp.arange(rows + 1, dtype=jnp.int32)[None, None, :, None, None]
    hidden = jnp.where((row_ids < rows) | (s < last), hidden, jnp.zeros_like(hidden))
    hpad = jnp.pad(hidden, ((0, 0), (0, 0), (0, 0), (0, 1), (0, 0)))
    hflat = hpad.reshape(clips * frames, rows + 1, width + 1, channels)

    kernel2 = down_weight.reshape(3, 3, channels, channels)
    latent = lax.conv_general_dilated(
        hflat,
        kernel2,
        window_strides=(2, 2),
        padding="VALID",
        dimension_numbers=("NHWC", "HWIO", "NHWC"),
        preferred_element_type=jnp.float32,
    ).astype(jnp.bfloat16)
    latent = latent.reshape(cotangent.shape)

    cflat = cotangent.reshape(clips * frames, rows // 2, width // 2, channels)
    grad_down = lax.conv_general_dilated(
        hflat,
        cflat,
        window_strides=(1, 1),
        padding="VALID",
        rhs_dilation=(2, 2),
        dimension_numbers=("CHWN", "IHWO", "NHWC"),
        preferred_element_type=jnp.float32,
    )
    grad_down = jnp.transpose(grad_down, (1, 2, 0, 3)).reshape(9 * channels, channels)

    cot2 = jnp.concatenate([cot_above, cotangent], axis=2).reshape(
        clips * frames, rows // 2 + 1, width // 2, channels
    )
    d_hidden = lax.conv_general_dilated(
        cot2,
        kernel2[::-1, ::-1],
        window_strides=(1, 1),
        padding=((0, 1), (2, 1)),
        lhs_dilation=(2, 2),
        dimension_numbers=("NHWC", "HWOI", "NHWC"),
        preferred_element_type=jnp.float32,
    ).reshape(clips, frames, rows, width, channels)

    d_conv = norm_back(conv_out[:, :, :rows], norm_gain, keeper, d_hidden)
    grad_conv = lax.conv_general_dilated(
        padded[:, :, : rows + 2],
        d_conv,
        window_strides=(1, 1, 1),
        padding="VALID",
        dimension_numbers=("CDHWN", "IDHWO", "NDHWC"),
        preferred_element_type=jnp.float32,
    )
    grad_conv = jnp.transpose(grad_conv, (1, 2, 3, 0, 4)).reshape(27 * channels, channels)

    grad_conv, grad_down = lax.psum((grad_conv, grad_down), ("tm", "space"))
    devices = lax.axis_size("tm") * lax.axis_size("space")
    me = t * lax.axis_size("space") + s
    conv_rows = grad_conv.shape[0] // devices
    down_rows = grad_down.shape[0] // devices
    conv_share = lax.dynamic_slice_in_dim(grad_conv, me * conv_rows, conv_rows, axis=0)
    down_share = lax.dynamic_slice_in_dim(grad_down, me * down_rows, down_rows, axis=0)
    return (latent, conv_share.reshape(-1), down_share.reshape(-1))


def solution(mesh):
    in_specs = (
        P(None, "tm", "space", None, None),
        P(),
        P(),
        P(),
        P(),
        P(None, "tm", "space", None, None),
    )
    out_specs = (P(None, "tm", "space", None, None), P(("tm", "space")), P(("tm", "space")))
    return jax.shard_map(local, mesh=mesh, in_specs=in_specs, out_specs=out_specs, check_vma=False)
```

time: 460 us -> 328 us (0.71)
  other arithmetic: 78.2 us -> 12.6 us
  matrix products: 68.8 us -> 29.5 us
  local copies, waits for them, and re-layouts: 53.2 us -> 19.7 us
    psum x0 -> x1, waiting for transfers between devices: none -> 228 us  [local(): grad_conv, grad_down = lax.psum((grad_conv, grad_down), ('tm', 'space'))]
    unnamed x2 -> x1, waiting for transfers between devices: 226 us -> 0.02 us
    dot_general x81 -> x0, matrix products: 68.8 us -> none  [the longest x27 32.3 us: conv_weight_grad(): jnp.dot(window.T, flat_grad, preferred_element_type=jnp.float32)]
    scatter-add x9 -> x0, other arithmetic: 45.9 us -> none  [down_back(): d_pad = d_pad.at[:, :, row_tap:row_tap + 2 * out_rows:2, col_tap:col_tap...]
    another operation x2 -> x0, local copies, waits for them, and re-layouts: 20.6 us -> none  [the longest x1 14.7 us: local(): grad_conv_term.reshape(devices, -1)]
    transpose x0 -> x2, matrix products: none -> 20.4 us  [the longest x1 16.9 us: local(): jnp.transpose(grad_conv, (1, 2, 3, 0, 4)).reshape(27 * channels, channels)]
    reshape x1 -> x6, local copies, waits for them, and re-layouts: 20 us -> 4.2 us  [the longest x2 2.79 us: local(): hflat = hpad.reshape(clips * frames, rows + 1, width + 1, channels)]
    concatenate x10 -> x2, other arithmetic: 18.4 us -> 4.44 us  [the longest x1 3.54 us: local(): jnp.concatenate([old, own], axis=1)]
  transfers between devices with their start and end apart: 6 -> 7, of which waited for: 2 -> 3; matrix products, arithmetic and copies ran while one was open for 30% -> 2% of each run, Pallas kernels for 0% -> 0%
where the time goes in v1:
time: 328 us
  waiting for transfers between devices  231 us (70%)
  matrix products  29.5 us (9%)
  starting transfers between devices  20.4 us (6%)
  local copies, waits for them, and re-layouts  19.7 us (6%)
  between operations  14.4 us (4%)
  other arithmetic  12.6 us (4%)
    psum x1, waiting for transfers between devices, local(): grad_conv, grad_down = lax.psum((grad_conv, grad_down), ('tm', 'space'))  228 us
    ppermute x6, starting transfers between devices, shifted(): return lax.ppermute(array, name, pairs)  20.3 us
    transpose x1, matrix products, local(): jnp.transpose(grad_conv, (1, 2, 3, 0, 4)).reshape(27 * channels, channels)  16.9 us
    conv_general_dilated x1, matrix products, local(): lax.conv_general_dilated(padded, kernel3, window_strides=(1, 1, 1), paddi...  7.46 us
  transfers between devices with their start and end apart: 7, of which 3 were waited for; matrix products, arithmetic and copies ran while one was open for 2% of the time, Pallas kernels for 0%

profile of v1, /device:TPU:1, one launch (start us, length us, event | category | flops | bytes accessed | tf_op | source)
XLA Modules:
  0.0 327.6 jit_solution(14497437829449106780)
XLA Ops:
  7.3 0.9 fusion.38
  8.1 2.0 copy_multiply_fusion
  10.2 1.7 slice.19
  11.8 4.9 %collective-permute-start.3 = (bf16[2,2,1,48,384]{4,0,3,2,1:T(2,128)(2,1)}, bf16[2,2,1,48,384]{4,0,3,2,1:T(2,128)(2,1)}, u32[]{:S(2)}, u32[]{:S(2)}) collective-permute-start(bf16[2,2,1,48,384]{4,0,3,2,1:T(2,128)(2,1)} %slice.19), channel_id=1, source_target_pairs={{0,1},{1,2},{2,3},{3,4},{4,5},{5,6},{6,7},{7,8},{8,9},{9,10},{10,1... | collective-permute-start | bytes 442376 | tf_op jit(solution)/shard_map/ppermute | solution.py:28
  16.8 3.5 %collective-permute-start = (bf16[2,2,1,48,384]{4,0,3,2,1:T(2,128)(2,1)}, bf16[2,2,1,48,384]{4,0,3,2,1:T(2,128)(2,1)}, u32[]{:S(2)}, u32[]{:S(2)}) collective-permute-start(bf16[2,2,1,48,384]{4,0,3,2,1:T(2,128)(2,1)} %slice.19), channel_id=1, source_target_pairs={{0,17},{1,18},{2,19},{3,20},{4,21},{5,22},{6,23},{7,24},{8,25},{9,... | collective-permute-start | bytes 442376 | tf_op jit(solution)/shard_map/ppermute | solution.py:28
  20.3 2.6 collective-permute-start.4
  22.8 3.1 collective-permute-start.2
  25.9 4.1 %collective-permute-start.5 = (bf16[2,2,1,24,384]{4,3,2,1,0:T(8,128)(2,1)}, bf16[2,2,1,24,384]{4,3,2,1,0:T(8,128)(2,1)S(1)}, u32[]{:S(2)}, u32[]{:S(2)}) collective-permute-start(bf16[2,2,1,24,384]{4,3,2,1,0:T(8,128)(2,1)} %param.11), channel_id=1, source_target_pairs={{0,1},{1,2},{2,3},{3,4},{4,5},{5,6},{6,7},{7,8},{8,9},{9,10},{10,1... | collective-permute-start | bytes 221192 | tf_op jit(solution)/shard_map/ppermute | solution.py:28
  30.1 0.7 convert_element_type.37
  30.8 0.9 collective-permute-done.5
  31.8 2.1 collective-permute-start.1
  33.9 0.9 pad_maximum_fusion
  35.1 1.0 convolution_select_fusion
  36.7 0.9 copy.53
  37.6 1.6 collective-permute-done.1
  39.2 0.7 copy-done.4
  39.9 3.5 %fusion.39 = bf16[4,5,2,48,384]{4,2,3,1,0:T(2,128)(2,1)S(1)} fusion(bf16[2,2,2,48,384]{4,0,3,2,1:T(2,128)(2,1)} %collective-permute-done.4, bf16[2,2,2,48,384]{4,0,3,2,1:T(2,128)(2,1)} %copy_multiply_fusion, bf16[2,2,1,48,384]{4,0,3,2,1:T(2,128)(2,1)} %collective-permute-done.3, bf16[2,2,2,48,384]{4,0,3,2,1:T(2,128)(2,1)} %collective-permute-done.2, ...), kind=kLoop, calls=%fused_computation.65 | loop fusion | flops 3686400 | bytes 2949120 | tf_op jit(solution)/shard_map/concatenate | solution.py:72
  43.4 1.3 pad.7
  45.6 7.5 %multiply_reduce_fusion = (f32[2,3,16,7]{2,3,1,0:T(8,128)S(1)}, f32[2,3,16,7,384]{4,2,3,1,0:T(8,128)S(1)}) fusion(bf16[3,3,3,384,384]{4,3,2,1,0:T(8,128)(2,1)S(1)} %bitcast.99, bf16[4,5,2,7,2,384]{5,3,2,4,1,0:T(8,128)(2,1)S(1)} %slice.20, bf16[4,5,2,8,7,384]{5,3,2,4,1,0:T(8,128)(2,1)S(1)} %copy.39, pred[16,7]{0,1:T(8,128)(4,1)S(1)} %copy-done.8), kind=kOutput, calls=%fused_computation.16 | convolution fusion | flops 5358292480 | bytes 11148016 | tf_op jit(solution)/shard_map/conv_general_dilated | solution.py:76
  53.0 0.9 multiply_reduce_fusion.1
  54.0 1.5 copy.40
  55.7 0.8 copy.42
  56.5 2.6 broadcast_select_fusion
  59.4 1.1 pad.6.clone
  60.5 2.6 reshape.128
  63.3 1.5 copy.55
  66.0 3.5 %fusion.30 = f32[3,3,384,384]{3,2,1,0:T(8,128)} fusion(bf16[4,3,49,384]{3,0,2,1:T(4,128)(2,1)S(1)} %copy-done.2, bf16[4,1,24,384]{3,2,0,1:T(8,128)(2,1)S(1)} %bitcast.96), kind=kOutput, calls=%fused_computation.46 | convolution fusion | flops 254803968 | bytes 5833728 | tf_op jit(solution)/shard_map/transpose | solution.py:111
  69.4 16.9 %fusion.25 = f32[3,3,3,384,384]{4,3,2,1,0:T(8,128)} fusion(bf16[2,2,2,48,384]{4,3,2,1,0:T(8,128)(2,1)S(1)} %multiply_convert_fusion.1, bf16[2,2,2,48,384]{4,0,3,2,1:T(2,128)(2,1)} %collective-permute-done.4, bf16[2,2,2,48,384]{4,0,3,2,1:T(2,128)(2,1)} %copy_multiply_fusion, bf16[2,2,1,48,384]{4,0,3,2,1:T(2,128)(2,1)} %collective-permute-done.3, ...), kind=kOutput, calls=%fused_computation.38 | convolution fusion | flops 3024027648 | bytes 17694720 | tf_op jit(solution)/shard_map/transpose | solution.py:135
  86.4 1.0 copy-done.3
  89.2 228.5 %all-reduce.4.cloned.1.call-done = (f32[10368,384]{1,0:T(8,128)}, f32[3456,384]{1,0:T(8,128)}) async-done(((f32[10368,384]{1,0:T(8,128)}, f32[3456,384]{1,0:T(8,128)}), (f32[10368,384]{1,0:T(8,128)}, f32[3456,384]{1,0:T(8,128)})) %all-reduce.4.cloned.1.call-update) | async-done | bytes 21233680 | tf_op jit(solution)/shard_map/psum | solution.py:137
  317.7 0.9 constant_dynamic-slice_fusion.1
  319.3 0.8 constant_dynamic-slice_fusion
  (63 shorter events, 6.7 us)
Async XLA Ops:
  7.2 27.9 %copy-start = (bf16[3456,384]{1,0:T(8,128)(2,1)S(1)}, bf16[3456,384]{1,0:T(8,128)(2,1)}, u32[]{:S(2)}) copy-start(bf16[3456,384]{1,0:T(8,128)(2,1)} %param.9) | copy-start | bytes 7962628
  7.2 27.9 %copy-start.7 = (pred[32,8]{0,1:T(8,128)(4,1)S(1)}, pred[32,8]{0,1:T(8,128)(4,1)}, u32[]{:S(2)}) copy-start(pred[32,8]{0,1:T(8,128)(4,1)} %constant.61) | copy-start | bytes 772
  7.2 310.5 %all-reduce.4.cloned.1.call-start = ((), (), s32[]{:S(2)}) async-start(), calls=%async_computation | async-start | bytes 42467328 | tf_op jit(solution)/shard_map/psum | solution.py:137
  11.8 25.7 %collective-permute-start.3 = (bf16[2,2,1,48,384]{4,0,3,2,1:T(2,128)(2,1)}, bf16[2,2,1,48,384]{4,0,3,2,1:T(2,128)(2,1)}, u32[]{:S(2)}, u32[]{:S(2)}) collective-permute-start(bf16[2,2,1,48,384]{4,0,3,2,1:T(2,128)(2,1)} %slice.19), channel_id=1, source_target_pairs={{0,1},{1,2},{2,3},{3,4},{4,5},{5,6},{6,7},{7,8},{8,9},{9,10},{10,1... | collective-permute-start | bytes 442376 | tf_op jit(solution)/shard_map/ppermute | solution.py:28
  16.8 20.8 %collective-permute-start = (bf16[2,2,1,48,384]{4,0,3,2,1:T(2,128)(2,1)}, bf16[2,2,1,48,384]{4,0,3,2,1:T(2,128)(2,1)}, u32[]{:S(2)}, u32[]{:S(2)}) collective-permute-start(bf16[2,2,1,48,384]{4,0,3,2,1:T(2,128)(2,1)} %slice.19), channel_id=1, source_target_pairs={{0,17},{1,18},{2,19},{3,20},{4,21},{5,22},{6,23},{7,24},{8,25},{9,... | collective-permute-start | bytes 442376 | tf_op jit(solution)/shard_map/ppermute | solution.py:28
  20.3 17.3 %collective-permute-start.4 = (bf16[2,2,2,48,384]{4,0,3,2,1:T(2,128)(2,1)}, bf16[2,2,2,48,384]{4,0,3,2,1:T(2,128)(2,1)}, u32[]{:S(2)}, u32[]{:S(2)}) collective-permute-start(bf16[2,2,2,48,384]{4,0,3,2,1:T(2,128)(2,1)} %copy_multiply_fusion), channel_id=1, source_target_pairs={{1,0},{2,1},{3,2},{4,3},{5,4},{6,5},{7,6},{8,7},{9,8},{10,9},{11,1... | collective-permute-start | bytes 884744 | tf_op jit(solution)/shard_map/ppermute | solution.py:28
  22.8 14.7 %collective-permute-start.2 = (bf16[2,2,2,48,384]{4,0,3,2,1:T(2,128)(2,1)}, bf16[2,2,2,48,384]{4,0,3,2,1:T(2,128)(2,1)}, u32[]{:S(2)}, u32[]{:S(2)}) collective-permute-start(bf16[2,2,2,48,384]{4,0,3,2,1:T(2,128)(2,1)} %copy_multiply_fusion), channel_id=1, source_target_pairs={{1,16},{2,17},{3,18},{4,19},{5,20},{6,21},{7,22},{8,23},{9,24},{10... | collective-permute-start | bytes 884744 | tf_op jit(solution)/shard_map/ppermute | solution.py:28
  25.9 5.8 %collective-permute-start.5 = (bf16[2,2,1,24,384]{4,3,2,1,0:T(8,128)(2,1)}, bf16[2,2,1,24,384]{4,3,2,1,0:T(8,128)(2,1)S(1)}, u32[]{:S(2)}, u32[]{:S(2)}) collective-permute-start(bf16[2,2,1,24,384]{4,3,2,1,0:T(8,128)(2,1)} %param.11), channel_id=1, source_target_pairs={{0,1},{1,2},{2,3},{3,4},{4,5},{5,6},{6,7},{7,8},{8,9},{9,10},{10,1... | collective-permute-start | bytes 221192 | tf_op jit(solution)/shard_map/ppermute | solution.py:28
  31.8 7.4 %collective-permute-start.1 = (bf16[2,2,2,48,384]{4,0,3,2,1:T(2,128)(2,1)}, bf16[2,2,2,48,384]{4,0,3,2,1:T(2,128)(2,1)S(1)}, u32[]{:S(2)}, u32[]{:S(2)}) collective-permute-start(bf16[2,2,2,48,384]{4,0,3,2,1:T(2,128)(2,1)} %copy_multiply_fusion), channel_id=1, source_target_pairs={{0,16},{16,32},{32,48},{48,64},{64,80},{80,96},{96,112},{1,17},{17... | collective-permute-start | bytes 884744 | tf_op jit(solution)/shard_map/ppermute | solution.py:28
  36.1 9.1 %slice-start = ((s8[7962624]{0:T(1024)(128)(4,1)}), s8[4194304]{0:T(1024)(128)(4,1)S(1)}, s32[]{:S(2)}) async-start(s8[7962624]{0:T(1024)(128)(4,1)} %bitcast.97), calls=%async_computation.1 | async-start | bytes 8388608
  39.2 0.7 copy-start.4
  43.4 2.1 slice-start.1
  44.7 0.8 copy-start.8
  63.3 1.8 copy-start.1
  64.8 1.1 copy-start.2
  64.8 1.1 copy-start.6
  66.0 3.5 %copy-start.5 = (bf16[2,2,2,48,384]{4,0,3,2,1:T(2,128)(2,1)S(1)}, bf16[2,2,2,48,384]{4,0,3,2,1:T(2,128)(2,1)}, u32[]{:S(2)}) copy-start(bf16[2,2,2,48,384]{4,0,3,2,1:T(2,128)(2,1)} %copy-done.4) | copy-start | bytes 884740
  86.4 1.0 copy-start.3
  86.4 1.5 copy-start.9
Sparse Core Ops, SparseCore 0:
  86.5 231.1 all-reduce.3

commit v2 on v1

--- a/solution.py
+++ b/solution.py
@@ -134,14 +134,20 @@
     )
     grad_conv = jnp.transpose(grad_conv, (1, 2, 3, 0, 4)).reshape(27 * channels, channels)
 
-    grad_conv, grad_down = lax.psum((grad_conv, grad_down), ("tm", "space"))
+    grad_conv, grad_down = lax.psum(
+        (grad_conv.astype(jnp.bfloat16), grad_down.astype(jnp.bfloat16)), ("tm", "space")
+    )
     devices = lax.axis_size("tm") * lax.axis_size("space")
     me = t * lax.axis_size("space") + s
     conv_rows = grad_conv.shape[0] // devices
     down_rows = grad_down.shape[0] // devices
     conv_share = lax.dynamic_slice_in_dim(grad_conv, me * conv_rows, conv_rows, axis=0)
     down_share = lax.dynamic_slice_in_dim(grad_down, me * down_rows, down_rows, axis=0)
-    return (latent, conv_share.reshape(-1), down_share.reshape(-1))
+    return (
+        latent,
+        conv_share.astype(jnp.float32).reshape(-1),
+        down_share.astype(jnp.float32).reshape(-1),
+    )
 
 
 def solution(mesh):

time: 328 us -> 265 us (0.81)
  waiting for transfers between devices: 231 us -> 170 us
  matrix products: 29.5 us -> 25.8 us
  other arithmetic: 12.6 us -> 16.1 us
    psum x1, waiting for transfers between devices: 228 us -> 168 us  [local(): lax.psum((grad_conv.astype(jnp.bfloat16), grad_down.astype(jnp.bfloat16))...]
    transpose x1, matrix products: 16.9 us -> 13.5 us  [local(): jnp.transpose(grad_conv, (1, 2, 3, 0, 4)).reshape(27 * channels, channels)]
  transfers between devices with their start and end apart: 7 -> 7, of which waited for: 3 -> 3; matrix products, arithmetic and copies ran while one was open for 2% -> 3% of each run, Pallas kernels for 0% -> 0%
where the time goes in v2:
time: 265 us
  waiting for transfers between devices  170 us (64%)
  matrix products  25.8 us (10%)
  starting transfers between devices  20.4 us (8%)
  local copies, waits for them, and re-layouts  18 us (7%)
  other arithmetic  16.1 us (6%)
  between operations  14.4 us (5%)
    psum x1, waiting for transfers between devices, local(): lax.psum((grad_conv.astype(jnp.bfloat16), grad_down.astype(jnp.bfloat16))...  168 us
    ppermute x6, starting transfers between devices, shifted(): return lax.ppermute(array, name, pairs)  20.3 us
    transpose x1, matrix products, local(): jnp.transpose(grad_conv, (1, 2, 3, 0, 4)).reshape(27 * channels, channels)  13.5 us
    conv_general_dilated x1, matrix products, local(): lax.conv_general_dilated(padded, kernel3, window_strides=(1, 1, 1), paddi...  7.46 us
  transfers between devices with their start and end apart: 7, of which 3 were waited for; matrix products, arithmetic and copies ran while one was open for 3% of the time, Pallas kernels for 0%

profile of v2, /device:TPU:1, one launch (start us, length us, event | category | flops | bytes accessed | tf_op | source)
XLA Modules:
  0.0 264.5 jit_solution(17978001176278147953)
XLA Ops:
  7.2 0.9 fusion.36
  8.1 2.1 copy_multiply_fusion
  10.2 1.7 slice.19
  11.9 4.9 %collective-permute-start.3 = (bf16[2,2,1,48,384]{4,0,3,2,1:T(2,128)(2,1)}, bf16[2,2,1,48,384]{4,0,3,2,1:T(2,128)(2,1)}, u32[]{:S(2)}, u32[]{:S(2)}) collective-permute-start(bf16[2,2,1,48,384]{4,0,3,2,1:T(2,128)(2,1)} %slice.19), channel_id=1, source_target_pairs={{0,1},{1,2},{2,3},{3,4},{4,5},{5,6},{6,7},{7,8},{8,9},{9,10},{10,1... | collective-permute-start | bytes 442376 | tf_op jit(solution)/shard_map/ppermute | solution.py:28
  16.8 3.5 %collective-permute-start = (bf16[2,2,1,48,384]{4,0,3,2,1:T(2,128)(2,1)}, bf16[2,2,1,48,384]{4,0,3,2,1:T(2,128)(2,1)}, u32[]{:S(2)}, u32[]{:S(2)}) collective-permute-start(bf16[2,2,1,48,384]{4,0,3,2,1:T(2,128)(2,1)} %slice.19), channel_id=1, source_target_pairs={{0,17},{1,18},{2,19},{3,20},{4,21},{5,22},{6,23},{7,24},{8,25},{9,... | collective-permute-start | bytes 442376 | tf_op jit(solution)/shard_map/ppermute | solution.py:28
  20.3 2.6 collective-permute-start.4
  22.9 3.1 %collective-permute-start.2 = (bf16[2,2,2,48,384]{4,0,3,2,1:T(2,128)(2,1)}, bf16[2,2,2,48,384]{4,0,3,2,1:T(2,128)(2,1)}, u32[]{:S(2)}, u32[]{:S(2)}) collective-permute-start(bf16[2,2,2,48,384]{4,0,3,2,1:T(2,128)(2,1)} %copy_multiply_fusion), channel_id=1, source_target_pairs={{1,16},{2,17},{3,18},{4,19},{5,20},{6,21},{7,22},{8,23},{9,24},{10... | collective-permute-start | bytes 884744 | tf_op jit(solution)/shard_map/ppermute | solution.py:28
  26.0 4.1 %collective-permute-start.5 = (bf16[2,2,1,24,384]{4,3,2,1,0:T(8,128)(2,1)}, bf16[2,2,1,24,384]{4,3,2,1,0:T(8,128)(2,1)S(1)}, u32[]{:S(2)}, u32[]{:S(2)}) collective-permute-start(bf16[2,2,1,24,384]{4,3,2,1,0:T(8,128)(2,1)} %param.11), channel_id=1, source_target_pairs={{0,1},{1,2},{2,3},{3,4},{4,5},{5,6},{6,7},{7,8},{8,9},{9,10},{10,1... | collective-permute-start | bytes 221192 | tf_op jit(solution)/shard_map/ppermute | solution.py:28
  31.8 2.1 collective-permute-start.1
  33.9 0.9 pad_maximum_fusion
  35.1 1.7 convolution_select_fusion
  37.4 0.9 copy.53
  38.3 1.1 collective-permute-done.1
  39.4 0.7 copy-done.4
  40.1 3.5 %fusion.42 = bf16[4,5,2,48,384]{4,2,3,1,0:T(2,128)(2,1)S(1)} fusion(bf16[2,2,2,48,384]{4,0,3,2,1:T(2,128)(2,1)} %collective-permute-done.4, bf16[2,2,2,48,384]{4,0,3,2,1:T(2,128)(2,1)} %copy_multiply_fusion, bf16[2,2,1,48,384]{4,0,3,2,1:T(2,128)(2,1)} %collective-permute-done.3, bf16[2,2,2,48,384]{4,0,3,2,1:T(2,128)(2,1)} %collective-permute-done.2, ...), kind=kLoop, calls=%fused_computation.65 | loop fusion | flops 3686400 | bytes 2949120 | tf_op jit(solution)/shard_map/concatenate | solution.py:72
  43.7 1.3 pad.7
  45.8 7.5 %multiply_reduce_fusion = (f32[2,3,16,7]{2,3,1,0:T(8,128)S(1)}, f32[2,3,16,7,384]{4,2,3,1,0:T(8,128)S(1)}) fusion(bf16[3,3,3,384,384]{4,3,2,1,0:T(8,128)(2,1)S(1)} %bitcast.100, bf16[4,5,2,7,2,384]{5,3,2,4,1,0:T(8,128)(2,1)S(1)} %slice.20, bf16[4,5,2,8,7,384]{5,3,2,4,1,0:T(8,128)(2,1)S(1)} %copy.39, pred[16,7]{0,1:T(8,128)(4,1)S(1)} %copy-done.8), kind=kOutput, calls=%fused_computation.18 | convolution fusion | flops 5358292480 | bytes 11148016 | tf_op jit(solution)/shard_map/conv_general_dilated | solution.py:76
  53.3 0.9 multiply_reduce_fusion.1
  54.2 1.5 copy.40
  56.0 0.8 copy.42
  56.7 2.6 broadcast_select_fusion
  59.7 1.1 pad.6.clone
  60.8 2.6 reshape.132
  63.6 1.5 copy.55
  65.3 1.1 multiply_reduce_fusion.2
  66.5 1.1 multiply_convert_fusion.1
  67.6 2.6 convolution_convert_fusion.1
  70.2 13.5 %convolution_convert_fusion = bf16[3,3,3,384,384]{4,3,2,1,0:T(8,128)(2,1)} fusion(bf16[2,2,2,48,384]{4,3,2,1,0:T(8,128)(2,1)S(1)} %multiply_convert_fusion.1, bf16[2,2,2,48,384]{4,0,3,2,1:T(2,128)(2,1)} %collective-permute-done.4, bf16[2,2,2,48,384]{4,0,3,2,1:T(2,128)(2,1)} %copy_multiply_fusion, bf16[2,2,1,48,384]{4,0,3,2,1:T(2,128)(2,1)} %collective-permute-done.3, ...), kind=kOutput, calls=%fused_computation | convolution fusion | flops 3028008960 | bytes 9732096 | tf_op jit(solution)/shard_map/transpose | solution.py:135
  83.7 1.0 copy-done.3
  86.5 168.2 %all-reduce.4.cloned.1.call-done = (bf16[10368,384]{1,0:T(8,128)(2,1)}, bf16[3456,384]{1,0:T(8,128)(2,1)}) async-done(((bf16[10368,384]{1,0:T(8,128)(2,1)}, bf16[3456,384]{1,0:T(8,128)(2,1)}), (bf16[10368,384]{1,0:T(8,128)(2,1)}, bf16[3456,384]{1,0:T(8,128)(2,1)})) %all-reduce.4.cloned.1.call-update) | async-done | bytes 10616848 | tf_op jit(solution)/shard_map/psum | solution.py:137
  254.7 0.9 dynamic-slice_convert_fusion
  256.3 0.8 dynamic-slice_convert_fusion.1
  (63 shorter events, 7.4 us)
Async XLA Ops:
  7.2 28.0 %copy-start = (bf16[3456,384]{1,0:T(8,128)(2,1)S(1)}, bf16[3456,384]{1,0:T(8,128)(2,1)}, u32[]{:S(2)}) copy-start(bf16[3456,384]{1,0:T(8,128)(2,1)} %param.9) | copy-start | bytes 7962628
  7.2 247.6 %all-reduce.4.cloned.1.call-start = ((), (), s32[]{:S(2)}) async-start(), calls=%async_computation | async-start | bytes 21233664 | tf_op jit(solution)/shard_map/psum | solution.py:137
  11.9 26.4 %collective-permute-start.3 = (bf16[2,2,1,48,384]{4,0,3,2,1:T(2,128)(2,1)}, bf16[2,2,1,48,384]{4,0,3,2,1:T(2,128)(2,1)}, u32[]{:S(2)}, u32[]{:S(2)}) collective-permute-start(bf16[2,2,1,48,384]{4,0,3,2,1:T(2,128)(2,1)} %slice.19), channel_id=1, source_target_pairs={{0,1},{1,2},{2,3},{3,4},{4,5},{5,6},{6,7},{7,8},{8,9},{9,10},{10,1... | collective-permute-start | bytes 442376 | tf_op jit(solution)/shard_map/ppermute | solution.py:28
  16.8 21.4 %collective-permute-start = (bf16[2,2,1,48,384]{4,0,3,2,1:T(2,128)(2,1)}, bf16[2,2,1,48,384]{4,0,3,2,1:T(2,128)(2,1)}, u32[]{:S(2)}, u32[]{:S(2)}) collective-permute-start(bf16[2,2,1,48,384]{4,0,3,2,1:T(2,128)(2,1)} %slice.19), channel_id=1, source_target_pairs={{0,17},{1,18},{2,19},{3,20},{4,21},{5,22},{6,23},{7,24},{8,25},{9,... | collective-permute-start | bytes 442376 | tf_op jit(solution)/shard_map/ppermute | solution.py:28
  20.3 17.9 %collective-permute-start.4 = (bf16[2,2,2,48,384]{4,0,3,2,1:T(2,128)(2,1)}, bf16[2,2,2,48,384]{4,0,3,2,1:T(2,128)(2,1)}, u32[]{:S(2)}, u32[]{:S(2)}) collective-permute-start(bf16[2,2,2,48,384]{4,0,3,2,1:T(2,128)(2,1)} %copy_multiply_fusion), channel_id=1, source_target_pairs={{1,0},{2,1},{3,2},{4,3},{5,4},{6,5},{7,6},{8,7},{9,8},{10,9},{11,1... | collective-permute-start | bytes 884744 | tf_op jit(solution)/shard_map/ppermute | solution.py:28
  22.9 15.4 %collective-permute-start.2 = (bf16[2,2,2,48,384]{4,0,3,2,1:T(2,128)(2,1)}, bf16[2,2,2,48,384]{4,0,3,2,1:T(2,128)(2,1)}, u32[]{:S(2)}, u32[]{:S(2)}) collective-permute-start(bf16[2,2,2,48,384]{4,0,3,2,1:T(2,128)(2,1)} %copy_multiply_fusion), channel_id=1, source_target_pairs={{1,16},{2,17},{3,18},{4,19},{5,20},{6,21},{7,22},{8,23},{9,24},{10... | collective-permute-start | bytes 884744 | tf_op jit(solution)/shard_map/ppermute | solution.py:28
  26.0 5.8 %collective-permute-start.5 = (bf16[2,2,1,24,384]{4,3,2,1,0:T(8,128)(2,1)}, bf16[2,2,1,24,384]{4,3,2,1,0:T(8,128)(2,1)S(1)}, u32[]{:S(2)}, u32[]{:S(2)}) collective-permute-start(bf16[2,2,1,24,384]{4,3,2,1,0:T(8,128)(2,1)} %param.11), channel_id=1, source_target_pairs={{0,1},{1,2},{2,3},{3,4},{4,5},{5,6},{6,7},{7,8},{8,9},{9,10},{10,1... | collective-permute-start | bytes 221192 | tf_op jit(solution)/shard_map/ppermute | solution.py:28
  30.2 26.5 %copy-start.7 = (f32[2,2]{1,0:T(2,128)}, f32[2,2]{1,0:T(2,128)S(1)}, u32[]{:S(2)}) copy-start(f32[2,2]{1,0:T(2,128)S(1)} %copy.43) | copy-start | bytes 52
  31.8 7.6 %collective-permute-start.1 = (bf16[2,2,2,48,384]{4,0,3,2,1:T(2,128)(2,1)}, bf16[2,2,2,48,384]{4,0,3,2,1:T(2,128)(2,1)S(1)}, u32[]{:S(2)}, u32[]{:S(2)}) collective-permute-start(bf16[2,2,2,48,384]{4,0,3,2,1:T(2,128)(2,1)} %copy_multiply_fusion), channel_id=1, source_target_pairs={{0,16},{16,32},{32,48},{48,64},{64,80},{80,96},{96,112},{1,17},{17... | collective-permute-start | bytes 884744 | tf_op jit(solution)/shard_map/ppermute | solution.py:28
  36.9 8.6 %slice-start = ((s8[7962624]{0:T(1024)(128)(4,1)}), s8[4194304]{0:T(1024)(128)(4,1)S(1)}, s32[]{:S(2)}) async-start(s8[7962624]{0:T(1024)(128)(4,1)} %bitcast.98), calls=%async_computation.1 | async-start | bytes 8388608
  39.4 0.7 copy-start.4
  43.7 2.1 slice-start.1
  45.0 0.8 copy-start.8
  63.4 4.1 %copy-start.6 = (bf16[2,2,1,24,384]{4,3,2,1,0:T(8,128)(2,1)S(1)}, bf16[2,2,1,24,384]{4,3,2,1,0:T(8,128)(2,1)}, u32[]{:S(2)}) copy-start(bf16[2,2,1,24,384]{4,3,2,1,0:T(8,128)(2,1)} %param.11) | copy-start | bytes 221188
  63.5 1.8 copy-start.1
  63.5 4.0 %copy-start.2 = (bf16[4,3,49,384]{3,0,2,1:T(4,128)(2,1)S(1)}, bf16[4,3,49,384]{3,0,2,1:T(4,128)(2,1)}, u32[]{:S(2)}) copy-start(bf16[4,3,49,384]{3,0,2,1:T(4,128)(2,1)} %reshape.132) | copy-start | bytes 1354756
  67.6 2.6 copy-start.5
  83.6 1.0 copy-start.3
  83.6 1.5 copy-start.9
Sparse Core Ops, SparseCore 0:
  83.8 170.8 all-reduce.3

commit v3 on v1

--- a/solution.py
+++ b/solution.py
@@ -59,12 +59,15 @@
     masked = video * keeper.astype(jnp.bfloat16)
 
     top = masked[:, :, rows - 1 :]
-    above = shifted(top, ("space",), (1,))
-    below = shifted(masked, ("space",), (-1,))
-    prev = shifted(masked, ("tm",), (1,))
-    prev_above = shifted(top, ("tm", "space"), (1, 1))
-    prev_below = shifted(masked, ("tm", "space"), (1, -1))
-    cot_above = shifted(cotangent, ("space",), (1,))
+    sent = jnp.concatenate([top, cotangent], axis=3)
+    got = shifted(sent.reshape(-1, channels), ("space",), (1,)).reshape(sent.shape)
+    above = got[:, :, :, :width]
+    cot_above = got[:, :, :, width:]
+    flat = masked.reshape(-1, channels)
+    below = shifted(flat, ("space",), (-1,)).reshape(masked.shape)
+    prev = shifted(flat, ("tm",), (1,)).reshape(masked.shape)
+    prev_above = shifted(top.reshape(-1, channels), ("tm", "space"), (1, 1)).reshape(top.shape)
+    prev_below = shifted(flat, ("tm", "space"), (1, -1)).reshape(masked.shape)
 
     own = jnp.concatenate([above, masked, below], axis=2)
     old = jnp.concatenate([prev_above, prev, prev_below], axis=2)

time: 328 us -> 322 us (0.982)
  local copies, waits for them, and re-layouts: 19.7 us -> 24.2 us
  starting transfers between devices: 20.4 us -> 16.3 us
  other arithmetic: 12.6 us -> 8.97 us
  matrix products: 29.5 us -> 26 us
    reshape x0 -> x4, local copies, waits for them, and re-layouts: none -> 4.64 us  [the longest x1 1.88 us: local(): below = shifted(flat, ('space',), (-1,)).reshape(masked.shape)]
    ppermute x6 -> x5, starting transfers between devices: 20.3 us -> 16.3 us  [shifted(): return lax.ppermute(array, name, pairs)]
    transpose x1, matrix products: 16.9 us -> 13.5 us  [local(): jnp.transpose(grad_conv, (1, 2, 3, 0, 4)).reshape(27 * channels, channels)]
  transfers between devices with their start and end apart: 7 -> 6, of which waited for: 3 -> 2; matrix products, arithmetic and copies ran while one was open for 2% -> 3% of each run, Pallas kernels for 0% -> 0%
where the time goes in v3:
time: 322 us
  waiting for transfers between devices  231 us (72%)
  matrix products  26 us (8%)
  local copies, waits for them, and re-layouts  24.2 us (8%)
  starting transfers between devices  16.3 us (5%)
  between operations  14.7 us (5%)
  other arithmetic  8.97 us (3%)
    psum x1, waiting for transfers between devices, local(): grad_conv, grad_down = lax.psum((grad_conv, grad_down), ('tm', 'space'))  231 us
    ppermute x5, starting transfers between devices, shifted(): return lax.ppermute(array, name, pairs)  16.3 us
    transpose x1, matrix products, local(): jnp.transpose(grad_conv, (1, 2, 3, 0, 4)).reshape(27 * channels, channels)  13.5 us
    conv_general_dilated x1, matrix products, local(): lax.conv_general_dilated(padded, kernel3, window_strides=(1, 1, 1), paddi...  7.46 us
  transfers between devices with their start and end apart: 6, of which 2 were waited for; matrix products, arithmetic and copies ran while one was open for 3% of the time, Pallas kernels for 0%

profile of v3, /device:TPU:1, one launch (start us, length us, event | category | flops | bytes accessed | tf_op | source)
XLA Modules:
  0.0 321.5 jit_solution(14626260463687243188)
XLA Ops:
  7.3 1.1 copy.56
  8.4 0.7 fusion.38
  9.1 1.3 copy_multiply_fusion
  10.9 4.9 %collective-permute-start.3 = (bf16[288,384]{1,0:T(8,128)(2,1)S(1)}, bf16[288,384]{1,0:T(8,128)(2,1)S(1)}, u32[]{:S(2)}, u32[]{:S(2)}) collective-permute-start(bf16[288,384]{1,0:T(8,128)(2,1)S(1)} %bitcast.105), channel_id=1, source_target_pairs={{0,1},{1,2},{2,3},{3,4},{4,5},{5,6},{6,7},{7,8},{8,9},{9,10},{10,1... | collective-permute-start | bytes 663560 | tf_op jit(solution)/shard_map/ppermute | solution.py:28
  15.9 2.9 collective-permute-start
  18.7 0.7 copy.52
  19.5 2.6 collective-permute-start.4
  22.0 3.1 collective-permute-start.2
  25.2 2.8 collective-permute-start.1
  28.6 1.0 convolution_select_fusion
  30.3 0.9 copy.77
  31.2 1.9 copy.59
  33.1 1.4 copy.55
  34.7 1.3 copy.54
  36.0 0.7 copy-done.10
  36.7 2.3 fusion.39
  39.0 1.3 pad.7
  41.1 7.5 %multiply_reduce_fusion = (f32[2,3,16,7]{2,3,1,0:T(8,128)S(1)}, f32[2,3,16,7,384]{4,2,3,1,0:T(8,128)S(1)}) fusion(bf16[3,3,3,384,384]{4,3,2,1,0:T(8,128)(2,1)S(1)} %bitcast.113, bf16[4,5,2,7,2,384]{5,3,2,4,1,0:T(8,128)(2,1)S(1)} %slice.29, bf16[4,5,2,8,7,384]{5,3,2,4,1,0:T(8,128)(2,1)S(1)} %copy.61, pred[16,7]{0,1:T(8,128)(4,1)S(1)} %copy-done.20), kind=kOutput, calls=%fused_computation.16 | convolution fusion | flops 5358292480 | bytes 11148016 | tf_op jit(solution)/shard_map/conv_general_dilated | solution.py:79
  48.6 0.9 multiply_reduce_fusion.1
  49.5 1.5 copy.62
  51.3 0.8 copy.64
  52.1 2.4 broadcast_select_fusion
  54.8 1.1 pad.6.clone
  56.0 2.6 reshape.160
  58.7 1.5 copy.79
  61.6 13.5 %fusion.25 = f32[3,3,3,384,384]{4,3,2,1,0:T(8,128)} fusion(bf16[2,2,2,48,384]{4,3,2,1,0:T(8,128)(2,1)S(1)} %multiply_convert_fusion.1, bf16[2,2,2,48,384]{4,0,3,2,1:T(2,128)(2,1)S(1)} %copy-done.7, bf16[2,2,2,48,384]{4,0,3,2,1:T(2,128)(2,1)S(1)} %copy-done.3, bf16[2,2,1,48,384]{4,0,3,2,1:T(2,128)(2,1)S(1)} %copy-done.15, ...), kind=kOutput, calls=%fused_computation.38 | convolution fusion | flops 3024027648 | bytes 17694720 | tf_op jit(solution)/shard_map/transpose | solution.py:138
  75.1 3.4 %fusion.30 = f32[3,3,384,384]{3,2,1,0:T(8,128)} fusion(bf16[4,3,49,384]{3,0,2,1:T(4,128)(2,1)S(1)} %copy-done.5, bf16[4,1,24,384]{3,2,0,1:T(8,128)(2,1)S(1)} %bitcast.104), kind=kOutput, calls=%fused_computation.46 | convolution fusion | flops 254803968 | bytes 5833728 | tf_op jit(solution)/shard_map/transpose | solution.py:114
  79.9 0.6 slice.33
  80.5 231.1 %all-reduce.4.cloned.1.call-done = (f32[10368,384]{1,0:T(8,128)}, f32[3456,384]{1,0:T(8,128)}) async-done(((f32[10368,384]{1,0:T(8,128)}, f32[3456,384]{1,0:T(8,128)}), (f32[10368,384]{1,0:T(8,128)}, f32[3456,384]{1,0:T(8,128)})) %all-reduce.4.cloned.1.call-update) | async-done | bytes 21233680 | tf_op jit(solution)/shard_map/psum | solution.py:140
  311.6 0.9 constant_dynamic-slice_fusion.1
  312.6 0.7 reshape.166
  313.2 0.8 constant_dynamic-slice_fusion
  (97 shorter events, 6.6 us)
Async XLA Ops:
  7.2 21.4 %copy-start = (bf16[3456,384]{1,0:T(8,128)(2,1)S(1)}, bf16[3456,384]{1,0:T(8,128)(2,1)}, u32[]{:S(2)}) copy-start(bf16[3456,384]{1,0:T(8,128)(2,1)} %param.9) | copy-start | bytes 7962628
  7.2 21.1 %copy-start.16 = (bf16[2,2,1,24,384]{4,3,2,1,0:T(8,128)(2,1)S(1)}, bf16[2,2,1,24,384]{4,3,2,1,0:T(8,128)(2,1)}, u32[]{:S(2)}) copy-start(bf16[2,2,1,24,384]{4,3,2,1,0:T(8,128)(2,1)} %param.11) | copy-start | bytes 221188
  7.2 20.9 %copy-start.19 = (bf16[384]{0:T(512)(128)(2,1)S(1)}, bf16[384]{0:T(512)(128)(2,1)}, u32[]{:S(2)}) copy-start(bf16[384]{0:T(512)(128)(2,1)} %param.8) | copy-start | bytes 2308
  7.2 304.4 %all-reduce.4.cloned.1.call-start = ((), (), s32[]{:S(2)}) async-start(), calls=%async_computation | async-start | bytes 42467328 | tf_op jit(solution)/shard_map/psum | solution.py:140
  9.1 19.5 %copy-start.18 = (pred[32,8]{0,1:T(8,128)(4,1)S(1)}, pred[32,8]{0,1:T(8,128)(4,1)}, u32[]{:S(2)}) copy-start(pred[32,8]{0,1:T(8,128)(4,1)} %constant.61) | copy-start | bytes 772
  10.4 8.3 %copy-start.1 = (bf16[2,2,2,48,384]{4,0,3,2,1:T(2,128)(2,1)}, bf16[2,2,2,48,384]{4,0,3,2,1:T(2,128)(2,1)S(1)}, u32[]{:S(2)}) copy-start(bf16[2,2,2,48,384]{4,0,3,2,1:T(2,128)(2,1)S(1)} %copy_multiply_fusion) | copy-start | bytes 884740
  10.9 17.3 %collective-permute-start.3 = (bf16[288,384]{1,0:T(8,128)(2,1)S(1)}, bf16[288,384]{1,0:T(8,128)(2,1)S(1)}, u32[]{:S(2)}, u32[]{:S(2)}) collective-permute-start(bf16[288,384]{1,0:T(8,128)(2,1)S(1)} %bitcast.105), channel_id=1, source_target_pairs={{0,1},{1,2},{2,3},{3,4},{4,5},{5,6},{6,7},{7,8},{8,9},{9,10},{10,1... | collective-permute-start | bytes 663560 | tf_op jit(solution)/shard_map/ppermute | solution.py:28
  15.9 12.2 %collective-permute-start = (bf16[192,384]{1,0:T(8,128)(2,1)S(1)}, bf16[192,384]{1,0:T(8,128)(2,1)S(1)}, u32[]{:S(2)}, u32[]{:S(2)}) collective-permute-start(bf16[192,384]{1,0:T(8,128)(2,1)S(1)} %bitcast.108), channel_id=1, source_target_pairs={{0,17},{1,18},{2,19},{3,20},{4,21},{5,22},{6,23},{7,24},{8,25},{9,... | collective-permute-start | bytes 442376 | tf_op jit(solution)/shard_map/ppermute | solution.py:28
  19.5 11.8 %collective-permute-start.4 = (bf16[384,384]{1,0:T(8,128)(2,1)}, bf16[384,384]{1,0:T(8,128)(2,1)}, u32[]{:S(2)}, u32[]{:S(2)}) collective-permute-start(bf16[384,384]{1,0:T(8,128)(2,1)} %bitcast.2), channel_id=1, source_target_pairs={{1,0},{2,1},{3,2},{4,3},{5,4},{6,5},{7,6},{8,7},{9,8},{10,9},{11,1... | collective-permute-start | bytes 884744 | tf_op jit(solution)/shard_map/ppermute | solution.py:28
  22.0 11.1 %collective-permute-start.2 = (bf16[384,384]{1,0:T(8,128)(2,1)}, bf16[384,384]{1,0:T(8,128)(2,1)}, u32[]{:S(2)}, u32[]{:S(2)}) collective-permute-start(bf16[384,384]{1,0:T(8,128)(2,1)} %bitcast.2), channel_id=1, source_target_pairs={{1,16},{2,17},{3,18},{4,19},{5,20},{6,21},{7,22},{8,23},{9,24},{10... | collective-permute-start | bytes 884744 | tf_op jit(solution)/shard_map/ppermute | solution.py:28
  25.2 9.5 %collective-permute-start.1 = (bf16[384,384]{1,0:T(8,128)(2,1)}, bf16[384,384]{1,0:T(8,128)(2,1)}, u32[]{:S(2)}, u32[]{:S(2)}) collective-permute-start(bf16[384,384]{1,0:T(8,128)(2,1)} %bitcast.2), channel_id=1, source_target_pairs={{0,16},{16,32},{32,48},{48,64},{64,80},{80,96},{96,112},{1,17},{17... | collective-permute-start | bytes 884744 | tf_op jit(solution)/shard_map/ppermute | solution.py:28
  28.2 7.8 %copy-start.12 = (bf16[2,2,1,48,384]{4,0,3,2,1:T(2,128)(2,1)}, bf16[2,2,1,48,384]{4,0,3,2,1:T(2,128)(2,1)S(1)}, u32[]{:S(2)}) copy-start(bf16[2,2,1,48,384]{4,0,3,2,1:T(2,128)(2,1)S(1)} %copy.53) | copy-start | bytes 442372
  29.8 6.2 %copy-start.14 = (bf16[2,2,1,48,384]{4,0,3,2,1:T(2,128)(2,1)}, bf16[2,2,1,48,384]{4,0,3,2,1:T(2,128)(2,1)S(1)}, u32[]{:S(2)}) copy-start(bf16[2,2,1,48,384]{4,0,3,2,1:T(2,128)(2,1)S(1)} %copy.84) | copy-start | bytes 442372
  30.3 6.5 %copy-start.2 = (bf16[2,2,2,48,384]{4,0,3,2,1:T(2,128)(2,1)S(1)}, bf16[2,2,2,48,384]{4,0,3,2,1:T(2,128)(2,1)}, u32[]{:S(2)}) copy-start(bf16[2,2,2,48,384]{4,0,3,2,1:T(2,128)(2,1)} %copy-done.1) | copy-start | bytes 884740
  30.3 10.5 %slice-start = ((s8[7962624]{0:T(1024)(128)(4,1)}), s8[4194304]{0:T(1024)(128)(4,1)S(1)}, s32[]{:S(2)}) async-start(s8[7962624]{0:T(1024)(128)(4,1)} %bitcast.111), calls=%async_computation.1 | async-start | bytes 8388608
  33.1 2.9 copy-start.6
  34.5 1.5 copy-start.8
  36.0 0.7 copy-start.10
  39.0 2.1 slice-start.1
  40.3 0.8 copy-start.20
  58.7 1.8 copy-start.4
  60.3 1.2 copy-start.3
  60.3 1.2 copy-start.7
  60.3 1.2 copy-start.9
  60.3 1.2 copy-start.11
  60.3 1.2 copy-start.13
  60.3 1.3 copy-start.15
  61.6 13.5 %copy-start.5 = (bf16[4,3,49,384]{3,0,2,1:T(4,128)(2,1)S(1)}, bf16[4,3,49,384]{3,0,2,1:T(4,128)(2,1)}, u32[]{:S(2)}) copy-start(bf16[4,3,49,384]{3,0,2,1:T(4,128)(2,1)} %reshape.160) | copy-start | bytes 1354756
  61.6 13.5 %copy-start.17 = (bf16[2,2,1,24,384]{4,3,2,1,0:T(8,128)(2,1)S(1)}, bf16[2,2,1,24,384]{4,3,2,1,0:T(8,128)(2,1)}, u32[]{:S(2)}) copy-start(bf16[2,2,1,24,384]{4,3,2,1,0:T(8,128)(2,1)} %param.11) | copy-start | bytes 221188
  78.5 0.7 copy-start.21
Sparse Core Ops, SparseCore 0:
  78.6 232.9 all-reduce.3

commit v4 on v3

--- a/solution.py
+++ b/solution.py
@@ -112,6 +112,7 @@
         preferred_element_type=jnp.float32,
     )
     grad_down = jnp.transpose(grad_down, (1, 2, 0, 3)).reshape(9 * channels, channels)
+    grad_down = lax.psum(grad_down, ("tm", "space"))
 
     cot2 = jnp.concatenate([cot_above, cotangent], axis=2).reshape(
         clips * frames, rows // 2 + 1, width // 2, channels
@@ -137,7 +138,8 @@
     )
     grad_conv = jnp.transpose(grad_conv, (1, 2, 3, 0, 4)).reshape(27 * channels, channels)
 
-    grad_conv, grad_down = lax.psum((grad_conv, grad_down), ("tm", "space"))
+    grad_down, grad_conv = lax.optimization_barrier((grad_down, grad_conv))
+    grad_conv = lax.psum(grad_conv, ("tm", "space"))
     devices = lax.axis_size("tm") * lax.axis_size("space")
     me = t * lax.axis_size("space") + s
     conv_rows = grad_conv.shape[0] // devices

time: 322 us -> 461 us (1.43)
  waiting for transfers between devices: 231 us -> 358 us
    psum x1 -> x2, waiting for transfers between devices: 231 us -> 358 us  [the longest x1 214 us: local(): grad_conv = lax.psum(grad_conv, ('tm', 'space'))]
  transfers between devices with their start and end apart: 6 -> 7, of which waited for: 2 -> 2; matrix products, arithmetic and copies ran while one was open for 3% -> 6% of each run, Pallas kernels for 0% -> 0%
where the time goes in v4:
time: 461 us; the launch traced here: 460 us
  waiting for transfers between devices  358 us (78%)
  matrix products  29.4 us (6%)
  local copies, waits for them, and re-layouts  28.7 us (6%)
  starting transfers between devices  16.4 us (4%)
  between operations  14.6 us (3%)
  other arithmetic  12.9 us (3%)
    psum x1, waiting for transfers between devices, local(): grad_conv = lax.psum(grad_conv, ('tm', 'space'))  214 us
    psum x1, waiting for transfers between devices, local(): grad_down = lax.psum(grad_down, ('tm', 'space'))  144 us
    transpose x1, matrix products, local(): jnp.transpose(grad_conv, (1, 2, 3, 0, 4)).reshape(27 * channels, channels)  16.9 us
    ppermute x5, starting transfers between devices, shifted(): return lax.ppermute(array, name, pairs)  16.3 us
  transfers between devices with their start and end apart: 7, of which 2 were waited for; matrix products, arithmetic and copies ran while one was open for 6% of the time, Pallas kernels for 0%

profile of v4, /device:TPU:1, one launch (start us, length us, event | category | flops | bytes accessed | tf_op | source)
XLA Modules:
  0.0 460.4 jit_solution(7538716591886111358)
XLA Ops:
  7.3 1.1 copy.56
  9.1 1.3 copy_multiply_fusion
  10.9 4.9 %collective-permute-start.3 = (bf16[288,384]{1,0:T(8,128)(2,1)S(1)}, bf16[288,384]{1,0:T(8,128)(2,1)S(1)}, u32[]{:S(2)}, u32[]{:S(2)}) collective-permute-start(bf16[288,384]{1,0:T(8,128)(2,1)S(1)} %bitcast.105), channel_id=1, source_target_pairs={{0,1},{1,2},{2,3},{3,4},{4,5},{5,6},{6,7},{7,8},{8,9},{9,10},{10,1... | collective-permute-start | bytes 663560 | tf_op jit(solution)/shard_map/ppermute | solution.py:28
  15.9 2.9 collective-permute-start
  19.5 2.6 collective-permute-start.4
  22.1 3.1 collective-permute-start.2
  25.2 2.8 collective-permute-start.1
  30.2 1.0 convolution_select_fusion
  32.0 0.9 copy.78
  32.8 1.9 copy.59
  34.8 1.4 copy.55
  36.2 1.4 copy.54
  38.3 2.3 fusion.39
  40.6 1.3 pad.7
  42.7 7.5 %multiply_reduce_fusion = (f32[2,3,16,7]{2,3,1,0:T(8,128)S(1)}, f32[2,3,16,7,384]{4,2,3,1,0:T(8,128)S(1)}) fusion(bf16[3,3,3,384,384]{4,3,2,1,0:T(8,128)(2,1)S(1)} %bitcast.113, bf16[4,5,2,7,2,384]{5,3,2,4,1,0:T(8,128)(2,1)S(1)} %slice.29, bf16[4,5,2,8,7,384]{5,3,2,4,1,0:T(8,128)(2,1)S(1)} %copy.61, pred[16,7]{0,1:T(8,128)(4,1)S(1)} %copy-done.18), kind=kOutput, calls=%fused_computation.16 | convolution fusion | flops 5358292480 | bytes 11148016 | tf_op jit(solution)/shard_map/conv_general_dilated | solution.py:79
  50.2 0.9 multiply_reduce_fusion.1
  51.1 1.5 copy.62
  53.4 0.9 reshape.180
  55.1 2.6 broadcast_select_fusion
  58.6 1.1 pad.6.clone
  59.7 2.6 reshape.160
  63.2 1.5 copy.80
  65.0 1.1 multiply_reduce_fusion.2
  66.1 1.8 multiply_convert_fusion.1
  67.9 3.4 fusion.30
  71.3 0.9 copy-done.3
  72.4 16.9 %fusion.25 = f32[3,3,3,384,384]{4,3,2,1,0:T(8,128)} fusion(bf16[2,2,2,48,384]{4,3,2,1,0:T(8,128)(2,1)} %multiply_convert_fusion.1, bf16[2,2,2,48,384]{4,0,3,2,1:T(2,128)(2,1)S(1)} %copy-done.8, bf16[2,2,2,48,384]{4,0,3,2,1:T(2,128)(2,1)S(1)} %copy-done.3, bf16[2,2,1,48,384]{4,0,3,2,1:T(2,128)(2,1)} %copy-done.13, ...), kind=kOutput, calls=%fused_computation.38 | convolution fusion | flops 3024027648 | bytes 17694720 | tf_op jit(solution)/shard_map/transpose | solution.py:139
  89.3 144.3 %all-reduce.4.cloned.1.call-done = f32[3456,384]{1,0:T(8,128)} async-done(((f32[3456,384]{1,0:T(8,128)}), f32[3456,384]{1,0:T(8,128)}) %all-reduce.4.cloned.1.call-update) | async-done | bytes 5308432 | tf_op jit(solution)/shard_map/psum | solution.py:115
  233.7 1.0 copy-done.6
  236.5 0.8 constant_dynamic-slice_fusion
  237.9 214.0 %all-reduce.6.cloned.1.call-done = f32[10368,384]{1,0:T(8,128)} async-done(((f32[10368,384]{1,0:T(8,128)}), f32[10368,384]{1,0:T(8,128)}) %all-reduce.6.cloned.1.call-update) | async-done | bytes 15925264 | tf_op jit(solution)/shard_map/psum | solution.py:142
  452.0 0.9 constant_dynamic-slice_fusion.1
  (96 shorter events, 13.3 us)
Async XLA Ops:
  7.2 23.1 %copy-start = (bf16[3456,384]{1,0:T(8,128)(2,1)S(1)}, bf16[3456,384]{1,0:T(8,128)(2,1)}, u32[]{:S(2)}) copy-start(bf16[3456,384]{1,0:T(8,128)(2,1)} %param.9) | copy-start | bytes 7962628
  7.2 22.7 %copy-start.14 = (bf16[2,2,1,24,384]{4,3,2,1,0:T(8,128)(2,1)S(1)}, bf16[2,2,1,24,384]{4,3,2,1,0:T(8,128)(2,1)}, u32[]{:S(2)}) copy-start(bf16[2,2,1,24,384]{4,3,2,1,0:T(8,128)(2,1)} %param.11) | copy-start | bytes 221188
  7.2 21.5 %copy-start.17 = (bf16[384]{0:T(512)(128)(2,1)S(1)}, bf16[384]{0:T(512)(128)(2,1)}, u32[]{:S(2)}) copy-start(bf16[384]{0:T(512)(128)(2,1)} %param.8) | copy-start | bytes 2308
  7.2 226.4 %all-reduce.4.cloned.1.call-start = ((), (), s32[]{:S(2)}) async-start(), calls=%async_computation | async-start | bytes 10616832 | tf_op jit(solution)/shard_map/psum | solution.py:115
  9.1 21.1 %copy-start.16 = (pred[32,8]{0,1:T(8,128)(4,1)S(1)}, pred[32,8]{0,1:T(8,128)(4,1)}, u32[]{:S(2)}) copy-start(pred[32,8]{0,1:T(8,128)(4,1)} %constant.61) | copy-start | bytes 772
  10.4 8.3 %copy-start.1 = (bf16[2,2,2,48,384]{4,0,3,2,1:T(2,128)(2,1)}, bf16[2,2,2,48,384]{4,0,3,2,1:T(2,128)(2,1)S(1)}, u32[]{:S(2)}) copy-start(bf16[2,2,2,48,384]{4,0,3,2,1:T(2,128)(2,1)S(1)} %copy_multiply_fusion) | copy-start | bytes 884740
  10.9 19.0 %collective-permute-start.3 = (bf16[288,384]{1,0:T(8,128)(2,1)S(1)}, bf16[288,384]{1,0:T(8,128)(2,1)S(1)}, u32[]{:S(2)}, u32[]{:S(2)}) collective-permute-start(bf16[288,384]{1,0:T(8,128)(2,1)S(1)} %bitcast.105), channel_id=1, source_target_pairs={{0,1},{1,2},{2,3},{3,4},{4,5},{5,6},{6,7},{7,8},{8,9},{9,10},{10,1... | collective-permute-start | bytes 663560 | tf_op jit(solution)/shard_map/ppermute | solution.py:28
  15.9 13.9 %collective-permute-start = (bf16[192,384]{1,0:T(8,128)(2,1)S(1)}, bf16[192,384]{1,0:T(8,128)(2,1)S(1)}, u32[]{:S(2)}, u32[]{:S(2)}) collective-permute-start(bf16[192,384]{1,0:T(8,128)(2,1)S(1)} %bitcast.108), channel_id=1, source_target_pairs={{0,17},{1,18},{2,19},{3,20},{4,21},{5,22},{6,23},{7,24},{8,25},{9,... | collective-permute-start | bytes 442376 | tf_op jit(solution)/shard_map/ppermute | solution.py:28
  19.5 13.4 %collective-permute-start.4 = (bf16[384,384]{1,0:T(8,128)(2,1)}, bf16[384,384]{1,0:T(8,128)(2,1)}, u32[]{:S(2)}, u32[]{:S(2)}) collective-permute-start(bf16[384,384]{1,0:T(8,128)(2,1)} %bitcast.2), channel_id=1, source_target_pairs={{1,0},{2,1},{3,2},{4,3},{5,4},{6,5},{7,6},{8,7},{9,8},{10,9},{11,1... | collective-permute-start | bytes 884744 | tf_op jit(solution)/shard_map/ppermute | solution.py:28
  22.1 12.7 %collective-permute-start.2 = (bf16[384,384]{1,0:T(8,128)(2,1)}, bf16[384,384]{1,0:T(8,128)(2,1)}, u32[]{:S(2)}, u32[]{:S(2)}) collective-permute-start(bf16[384,384]{1,0:T(8,128)(2,1)} %bitcast.2), channel_id=1, source_target_pairs={{1,16},{2,17},{3,18},{4,19},{5,20},{6,21},{7,22},{8,23},{9,24},{10... | collective-permute-start | bytes 884744 | tf_op jit(solution)/shard_map/ppermute | solution.py:28
  25.2 11.0 %collective-permute-start.1 = (bf16[384,384]{1,0:T(8,128)(2,1)}, bf16[384,384]{1,0:T(8,128)(2,1)}, u32[]{:S(2)}, u32[]{:S(2)}) collective-permute-start(bf16[384,384]{1,0:T(8,128)(2,1)} %bitcast.2), channel_id=1, source_target_pairs={{0,16},{16,32},{32,48},{48,64},{64,80},{80,96},{96,112},{1,17},{17... | collective-permute-start | bytes 884744 | tf_op jit(solution)/shard_map/ppermute | solution.py:28
  29.9 7.7 %copy-start.12 = (bf16[2,2,1,48,384]{4,0,3,2,1:T(2,128)(2,1)}, bf16[2,2,1,48,384]{4,0,3,2,1:T(2,128)(2,1)S(1)}, u32[]{:S(2)}) copy-start(bf16[2,2,1,48,384]{4,0,3,2,1:T(2,128)(2,1)S(1)} %copy.53) | copy-start | bytes 442372
  31.4 6.1 %copy-start.13 = (bf16[2,2,1,48,384]{4,0,3,2,1:T(2,128)(2,1)}, bf16[2,2,1,48,384]{4,0,3,2,1:T(2,128)(2,1)S(1)}, u32[]{:S(2)}) copy-start(bf16[2,2,1,48,384]{4,0,3,2,1:T(2,128)(2,1)S(1)} %copy.84) | copy-start | bytes 442372
  31.9 6.4 %copy-start.2 = (bf16[2,2,2,48,384]{4,0,3,2,1:T(2,128)(2,1)S(1)}, bf16[2,2,2,48,384]{4,0,3,2,1:T(2,128)(2,1)}, u32[]{:S(2)}) copy-start(bf16[2,2,2,48,384]{4,0,3,2,1:T(2,128)(2,1)} %copy-done.1) | copy-start | bytes 884740
  31.9 10.4 %slice-start = ((s8[7962624]{0:T(1024)(128)(4,1)}), s8[4194304]{0:T(1024)(128)(4,1)S(1)}, s32[]{:S(2)}) async-start(s8[7962624]{0:T(1024)(128)(4,1)} %bitcast.111), calls=%async_computation.2 | async-start | bytes 8388608
  34.8 2.8 copy-start.7
  36.1 1.4 copy-start.9
  37.6 0.7 copy-start.11
  40.6 2.1 slice-start.1
  41.9 0.8 copy-start.18
  58.6 6.3 %copy-start.15 = (f32[384]{0:T(512)S(1)}, f32[384]{0:T(512)}, u32[]{:S(2)}) copy-start(f32[384]{0:T(512)} %convert_element_type.37) | copy-start | bytes 4612
  63.2 1.8 copy-start.4
  64.7 3.1 copy-start.5
  71.2 1.0 copy-start.3
  71.3 1.0 copy-start.8
  71.3 1.1 copy-start.10
  71.3 380.7 %all-reduce.6.cloned.1.call-start = ((), (), s32[]{:S(2)}) async-start(), calls=%async_computation.1 | async-start | bytes 31850496 | tf_op jit(solution)/shard_map/psum | solution.py:142
  233.6 1.0 copy-start.6
  233.7 1.5 copy-start.19
Sparse Core Ops, SparseCore 0:
  71.4 162.1 all-reduce.3
  239.0 212.8 all-reduce.5

commit v5 on v3

--- a/solution.py
+++ b/solution.py
@@ -56,21 +56,24 @@
     keeper = (frame_ids[None, :] < clip_lengths[:, None]).astype(jnp.float32)[
         :, :, None, None, None
     ]
-    masked = video * keeper.astype(jnp.bfloat16)
+    prev_ids = frame_ids - frames
+    prev_keeper = (prev_ids[None, :] < clip_lengths[:, None]).astype(jnp.bfloat16)[
+        :, :, None, None, None
+    ]
 
-    top = masked[:, :, rows - 1 :]
+    top = video[:, :, rows - 1 :]
     sent = jnp.concatenate([top, cotangent], axis=3)
     got = shifted(sent.reshape(-1, channels), ("space",), (1,)).reshape(sent.shape)
     above = got[:, :, :, :width]
     cot_above = got[:, :, :, width:]
-    flat = masked.reshape(-1, channels)
-    below = shifted(flat, ("space",), (-1,)).reshape(masked.shape)
-    prev = shifted(flat, ("tm",), (1,)).reshape(masked.shape)
+    flat = video.reshape(-1, channels)
+    below = shifted(flat, ("space",), (-1,)).reshape(video.shape)
+    prev = shifted(flat, ("tm",), (1,)).reshape(video.shape)
     prev_above = shifted(top.reshape(-1, channels), ("tm", "space"), (1, 1)).reshape(top.shape)
-    prev_below = shifted(flat, ("tm", "space"), (1, -1)).reshape(masked.shape)
+    prev_below = shifted(flat, ("tm", "space"), (1, -1)).reshape(video.shape)
 
-    own = jnp.concatenate([above, masked, below], axis=2)
-    old = jnp.concatenate([prev_above, prev, prev_below], axis=2)
+    own = jnp.concatenate([above, video, below], axis=2) * keeper.astype(jnp.bfloat16)
+    old = jnp.concatenate([prev_above, prev, prev_below], axis=2) * prev_keeper
     padded = jnp.pad(
         jnp.concatenate([old, own], axis=1), ((0, 0), (0, 0), (0, 0), (1, 1), (0, 0))
     )

time: 322 us -> 324 us (level)
  transfers between devices with their start and end apart: 6 -> 6, of which waited for: 2 -> 1; matrix products, arithmetic and copies ran while one was open for 3% -> 4% of each run, Pallas kernels for 0% -> 0%
where the time goes in v5:
time: 324 us; the launch traced here: 323 us
  waiting for transfers between devices  230 us (71%)
  matrix products  25.7 us (8%)
  local copies, waits for them, and re-layouts  24.6 us (8%)
  starting transfers between devices  16.4 us (5%)
  between operations  14.5 us (4%)
  other arithmetic  12.2 us (4%)
    psum x1, waiting for transfers between devices, local(): grad_conv, grad_down = lax.psum((grad_conv, grad_down), ('tm', 'space'))  230 us
    ppermute x5, starting transfers between devices, shifted(): return lax.ppermute(array, name, pairs)  16.4 us
    transpose x1, matrix products, local(): jnp.transpose(grad_conv, (1, 2, 3, 0, 4)).reshape(27 * channels, channels)  13.2 us
    conv_general_dilated x1, matrix products, local(): lax.conv_general_dilated(padded, kernel3, window_strides=(1, 1, 1), paddi...  7.46 us
  transfers between devices with their start and end apart: 6, of which 1 were waited for; matrix products, arithmetic and copies ran while one was open for 4% of the time, Pallas kernels for 0%

profile of v5, /device:TPU:1, one launch (start us, length us, event | category | flops | bytes accessed | tf_op | source)
XLA Modules:
  0.0 323.1 jit_solution(11762050784595273504)
XLA Ops:
  7.2 3.4 %collective-permute-start.4 = (bf16[384,384]{1,0:T(8,128)(2,1)}, bf16[384,384]{1,0:T(8,128)(2,1)}, u32[]{:S(2)}, u32[]{:S(2)}) collective-permute-start(bf16[384,384]{1,0:T(8,128)(2,1)} %bitcast.102), channel_id=1, source_target_pairs={{1,0},{2,1},{3,2},{4,3},{5,4},{6,5},{7,6},{8,7},{9,8},{10,9},{11,1... | collective-permute-start | bytes 884744 | tf_op jit(solution)/shard_map/ppermute | solution.py:28
  10.7 3.2 collective-permute-start.2
  13.9 3.1 collective-permute-start.1
  17.0 0.9 slice.13
  17.9 4.3 %collective-permute-start = (bf16[192,384]{1,0:T(8,128)(2,1)S(1)}, bf16[192,384]{1,0:T(8,128)(2,1)S(1)}, u32[]{:S(2)}, u32[]{:S(2)}) collective-permute-start(bf16[192,384]{1,0:T(8,128)(2,1)S(1)} %bitcast.105), channel_id=1, source_target_pairs={{0,17},{1,18},{2,19},{3,20},{4,21},{5,22},{6,23},{7,24},{8,25},{9,... | collective-permute-start | bytes 442376 | tf_op jit(solution)/shard_map/ppermute | solution.py:28
  22.3 0.9 pad_maximum_fusion.1
  23.2 2.3 collective-permute-start.3
  26.2 2.0 copy.49
  29.1 0.9 pad_maximum_fusion.2
  30.4 1.0 convolution_select_fusion
  32.1 0.9 copy.68
  32.9 1.3 copy.50
  34.2 1.4 copy.47
  35.6 1.3 copy.46
  36.9 1.4 maximum_multiply_fusion.1
  38.3 1.2 maximum_multiply_fusion
  39.5 0.9 copy-done.3
  40.4 1.9 fusion.39
  42.3 1.3 pad.7
  44.4 7.5 %multiply_reduce_fusion = (f32[2,3,16,7]{2,3,1,0:T(8,128)S(1)}, f32[2,3,16,7,384]{4,2,3,1,0:T(8,128)S(1)}) fusion(bf16[3,3,3,384,384]{4,3,2,1,0:T(8,128)(2,1)S(1)} %bitcast.116, bf16[4,5,2,7,2,384]{5,3,2,4,1,0:T(8,128)(2,1)S(1)} %slice.28, bf16[4,5,2,8,7,384]{5,3,2,4,1,0:T(8,128)(2,1)S(1)} %copy.52, pred[16,7]{0,1:T(8,128)(4,1)S(1)} %copy-done.10), kind=kOutput, calls=%fused_computation.16 | convolution fusion | flops 5358292480 | bytes 11148016 | tf_op jit(solution)/shard_map/conv_general_dilated | solution.py:82
  51.9 0.9 multiply_reduce_fusion.1
  52.8 1.5 copy.53
  54.5 0.8 copy.55
  55.3 2.6 broadcast_select_fusion
  58.3 1.1 pad.6.clone
  59.4 2.6 reshape.190
  62.2 1.6 copy.70
  64.9 13.2 %fusion.25 = f32[3,3,3,384,384]{4,3,2,1,0:T(8,128)} fusion(bf16[2,2,2,48,384]{4,3,2,1,0:T(8,128)(2,1)S(1)} %multiply_convert_fusion.1, bf16[2,2,5,48,384]{4,0,3,2,1:T(2,128)(2,1)S(1)} %copy-done.2, bf16[2,2,5,48,384]{4,0,3,2,1:T(2,128)(2,1)S(1)} %copy-done.4), kind=kOutput, calls=%fused_computation.40 | convolution fusion | flops 3018129408 | bytes 17694720 | tf_op jit(solution)/shard_map/transpose | solution.py:141
  78.1 3.4 %fusion.30 = f32[3,3,384,384]{3,2,1,0:T(8,128)} fusion(bf16[4,3,49,384]{3,0,2,1:T(4,128)(2,1)S(1)} %copy-done.6, bf16[4,1,24,384]{3,2,0,1:T(8,128)(2,1)S(1)} %bitcast.108), kind=kOutput, calls=%fused_computation.47 | convolution fusion | flops 254803968 | bytes 5833728 | tf_op jit(solution)/shard_map/transpose | solution.py:117
  83.5 229.7 %all-reduce.4.cloned.1.call-done = (f32[10368,384]{1,0:T(8,128)}, f32[3456,384]{1,0:T(8,128)}) async-done(((f32[10368,384]{1,0:T(8,128)}, f32[3456,384]{1,0:T(8,128)}), (f32[10368,384]{1,0:T(8,128)}, f32[3456,384]{1,0:T(8,128)})) %all-reduce.4.cloned.1.call-update) | async-done | bytes 21233680 | tf_op jit(solution)/shard_map/psum | solution.py:143
  313.2 0.9 constant_dynamic-slice_fusion.1
  314.8 0.8 constant_dynamic-slice_fusion
  (75 shorter events, 8.5 us)
Async XLA Ops:
  7.2 23.2 %copy-start = (bf16[3456,384]{1,0:T(8,128)(2,1)S(1)}, bf16[3456,384]{1,0:T(8,128)(2,1)}, u32[]{:S(2)}) copy-start(bf16[3456,384]{1,0:T(8,128)(2,1)} %param.9) | copy-start | bytes 7962628
  7.2 23.2 %copy-start.9 = (pred[32,8]{0,1:T(8,128)(4,1)S(1)}, pred[32,8]{0,1:T(8,128)(4,1)}, u32[]{:S(2)}) copy-start(pred[32,8]{0,1:T(8,128)(4,1)} %constant.64) | copy-start | bytes 772
  7.2 306.1 %all-reduce.4.cloned.1.call-start = ((), (), s32[]{:S(2)}) async-start(), calls=%async_computation | async-start | bytes 42467328 | tf_op jit(solution)/shard_map/psum | solution.py:143
  7.2 25.7 %collective-permute-start.4 = (bf16[384,384]{1,0:T(8,128)(2,1)}, bf16[384,384]{1,0:T(8,128)(2,1)}, u32[]{:S(2)}, u32[]{:S(2)}) collective-permute-start(bf16[384,384]{1,0:T(8,128)(2,1)} %bitcast.102), channel_id=1, source_target_pairs={{1,0},{2,1},{3,2},{4,3},{5,4},{6,5},{7,6},{8,7},{9,8},{10,9},{11,1... | collective-permute-start | bytes 884744 | tf_op jit(solution)/shard_map/ppermute | solution.py:28
  10.7 23.5 %collective-permute-start.2 = (bf16[384,384]{1,0:T(8,128)(2,1)}, bf16[384,384]{1,0:T(8,128)(2,1)}, u32[]{:S(2)}, u32[]{:S(2)}) collective-permute-start(bf16[384,384]{1,0:T(8,128)(2,1)} %bitcast.103), channel_id=1, source_target_pairs={{1,16},{2,17},{3,18},{4,19},{5,20},{6,21},{7,22},{8,23},{9,24},{10... | collective-permute-start | bytes 884744 | tf_op jit(solution)/shard_map/ppermute | solution.py:28
  13.9 21.8 %collective-permute-start.1 = (bf16[384,384]{1,0:T(8,128)(2,1)}, bf16[384,384]{1,0:T(8,128)(2,1)}, u32[]{:S(2)}, u32[]{:S(2)}) collective-permute-start(bf16[384,384]{1,0:T(8,128)(2,1)} %bitcast.104), channel_id=1, source_target_pairs={{0,16},{16,32},{32,48},{48,64},{64,80},{80,96},{96,112},{1,17},{17... | collective-permute-start | bytes 884744 | tf_op jit(solution)/shard_map/ppermute | solution.py:28
  17.9 11.0 %collective-permute-start = (bf16[192,384]{1,0:T(8,128)(2,1)S(1)}, bf16[192,384]{1,0:T(8,128)(2,1)S(1)}, u32[]{:S(2)}, u32[]{:S(2)}) collective-permute-start(bf16[192,384]{1,0:T(8,128)(2,1)S(1)} %bitcast.105), channel_id=1, source_target_pairs={{0,17},{1,18},{2,19},{3,20},{4,21},{5,22},{6,23},{7,24},{8,25},{9,... | collective-permute-start | bytes 442376 | tf_op jit(solution)/shard_map/ppermute | solution.py:28
  23.2 5.9 %collective-permute-start.3 = (bf16[288,384]{1,0:T(8,128)(2,1)S(1)}, bf16[288,384]{1,0:T(8,128)(2,1)S(1)}, u32[]{:S(2)}, u32[]{:S(2)}) collective-permute-start(bf16[288,384]{1,0:T(8,128)(2,1)S(1)} %bitcast.109), channel_id=1, source_target_pairs={{0,1},{1,2},{2,3},{3,4},{4,5},{5,6},{6,7},{7,8},{8,9},{9,10},{10,1... | collective-permute-start | bytes 663560 | tf_op jit(solution)/shard_map/ppermute | solution.py:28
  31.5 5.4 %copy-start.7 = (bf16[2,2,2,48,384]{4,0,3,2,1:T(2,128)(2,1)S(1)}, bf16[2,2,2,48,384]{4,0,3,2,1:T(2,128)(2,1)}, u32[]{:S(2)}) copy-start(bf16[2,2,2,48,384]{4,0,3,2,1:T(2,128)(2,1)} %copy.49) | copy-start | bytes 884740
  34.2 9.8 %slice-start = ((s8[7962624]{0:T(1024)(128)(4,1)}), s8[4194304]{0:T(1024)(128)(4,1)S(1)}, s32[]{:S(2)}) async-start(s8[7962624]{0:T(1024)(128)(4,1)} %bitcast.114), calls=%async_computation.1 | async-start | bytes 8388608
  38.3 1.2 copy-start.1
  39.5 0.9 copy-start.3
  42.3 2.1 slice-start.1
  43.6 0.8 copy-start.10
  62.1 1.9 copy-start.5
  62.2 2.7 copy-start.2
  62.2 2.7 copy-start.4
  64.9 13.2 %copy-start.6 = (bf16[4,3,49,384]{3,0,2,1:T(4,128)(2,1)S(1)}, bf16[4,3,49,384]{3,0,2,1:T(4,128)(2,1)}, u32[]{:S(2)}) copy-start(bf16[4,3,49,384]{3,0,2,1:T(4,128)(2,1)} %reshape.190) | copy-start | bytes 1354756
  64.9 13.2 %copy-start.8 = (bf16[2,2,1,24,384]{4,3,2,1,0:T(8,128)(2,1)S(1)}, bf16[2,2,1,24,384]{4,3,2,1,0:T(8,128)(2,1)}, u32[]{:S(2)}) copy-start(bf16[2,2,1,24,384]{4,3,2,1,0:T(8,128)(2,1)} %param.11) | copy-start | bytes 221188
  81.5 0.7 copy-start.11
Sparse Core Ops, SparseCore 0:
  81.7 231.5 all-reduce.3

commit v6 on v3

--- a/solution.py
+++ b/solution.py
@@ -137,7 +137,7 @@
     )
     grad_conv = jnp.transpose(grad_conv, (1, 2, 3, 0, 4)).reshape(27 * channels, channels)
 
-    grad_conv, grad_down = lax.psum((grad_conv, grad_down), ("tm", "space"))
+    grad_conv, grad_down = lax.psum((grad_conv, grad_down), ("space", "tm"))
     devices = lax.axis_size("tm") * lax.axis_size("space")
     me = t * lax.axis_size("space") + s
     conv_rows = grad_conv.shape[0] // devices

time: 322 us -> 322 us (level)
  no operation moved by 1% of the time
where the time goes in v6:
time: 322 us
  waiting for transfers between devices  231 us (72%)
  matrix products  26 us (8%)
  local copies, waits for them, and re-layouts  24.2 us (8%)
  starting transfers between devices  16.3 us (5%)
  between operations  14.7 us (5%)
  other arithmetic  8.97 us (3%)
    psum x1, waiting for transfers between devices, local(): grad_conv, grad_down = lax.psum((grad_conv, grad_down), ('space', 'tm'))  231 us
    ppermute x5, starting transfers between devices, shifted(): return lax.ppermute(array, name, pairs)  16.3 us
    transpose x1, matrix products, local(): jnp.transpose(grad_conv, (1, 2, 3, 0, 4)).reshape(27 * channels, channels)  13.5 us
    conv_general_dilated x1, matrix products, local(): lax.conv_general_dilated(padded, kernel3, window_strides=(1, 1, 1), paddi...  7.46 us
  transfers between devices with their start and end apart: 6, of which 2 were waited for; matrix products, arithmetic and copies ran while one was open for 3% of the time, Pallas kernels for 0%

profile of v6, /device:TPU:1, one launch (start us, length us, event | category | flops | bytes accessed | tf_op | source)
XLA Modules:
  0.0 321.5 jit_solution(14626260463687243188)
XLA Ops:
  7.3 1.1 copy.56
  8.4 0.7 fusion.38
  9.1 1.3 copy_multiply_fusion
  10.9 4.9 %collective-permute-start.3 = (bf16[288,384]{1,0:T(8,128)(2,1)S(1)}, bf16[288,384]{1,0:T(8,128)(2,1)S(1)}, u32[]{:S(2)}, u32[]{:S(2)}) collective-permute-start(bf16[288,384]{1,0:T(8,128)(2,1)S(1)} %bitcast.105), channel_id=1, source_target_pairs={{0,1},{1,2},{2,3},{3,4},{4,5},{5,6},{6,7},{7,8},{8,9},{9,10},{10,1... | collective-permute-start | bytes 663560 | tf_op jit(solution)/shard_map/ppermute | solution.py:28
  15.9 2.9 collective-permute-start
  18.7 0.7 copy.52
  19.5 2.6 collective-permute-start.4
  22.0 3.1 collective-permute-start.2
  25.2 2.8 collective-permute-start.1
  28.6 1.0 convolution_select_fusion
  30.3 0.9 copy.77
  31.2 1.9 copy.59
  33.1 1.4 copy.55
  34.7 1.3 copy.54
  36.0 0.7 copy-done.10
  36.7 2.3 fusion.39
  39.0 1.3 pad.7
  41.1 7.5 %multiply_reduce_fusion = (f32[2,3,16,7]{2,3,1,0:T(8,128)S(1)}, f32[2,3,16,7,384]{4,2,3,1,0:T(8,128)S(1)}) fusion(bf16[3,3,3,384,384]{4,3,2,1,0:T(8,128)(2,1)S(1)} %bitcast.113, bf16[4,5,2,7,2,384]{5,3,2,4,1,0:T(8,128)(2,1)S(1)} %slice.29, bf16[4,5,2,8,7,384]{5,3,2,4,1,0:T(8,128)(2,1)S(1)} %copy.61, pred[16,7]{0,1:T(8,128)(4,1)S(1)} %copy-done.20), kind=kOutput, calls=%fused_computation.16 | convolution fusion | flops 5358292480 | bytes 11148016 | tf_op jit(solution)/shard_map/conv_general_dilated | solution.py:79
  48.6 0.9 multiply_reduce_fusion.1
  49.5 1.5 copy.62
  51.3 0.8 copy.64
  52.1 2.4 broadcast_select_fusion
  54.8 1.1 pad.6.clone
  56.0 2.6 reshape.160
  58.7 1.5 copy.79
  61.6 13.5 %fusion.25 = f32[3,3,3,384,384]{4,3,2,1,0:T(8,128)} fusion(bf16[2,2,2,48,384]{4,3,2,1,0:T(8,128)(2,1)S(1)} %multiply_convert_fusion.1, bf16[2,2,2,48,384]{4,0,3,2,1:T(2,128)(2,1)S(1)} %copy-done.7, bf16[2,2,2,48,384]{4,0,3,2,1:T(2,128)(2,1)S(1)} %copy-done.3, bf16[2,2,1,48,384]{4,0,3,2,1:T(2,128)(2,1)S(1)} %copy-done.15, ...), kind=kOutput, calls=%fused_computation.38 | convolution fusion | flops 3024027648 | bytes 17694720 | tf_op jit(solution)/shard_map/transpose | solution.py:138
  75.1 3.4 %fusion.30 = f32[3,3,384,384]{3,2,1,0:T(8,128)} fusion(bf16[4,3,49,384]{3,0,2,1:T(4,128)(2,1)S(1)} %copy-done.5, bf16[4,1,24,384]{3,2,0,1:T(8,128)(2,1)S(1)} %bitcast.104), kind=kOutput, calls=%fused_computation.46 | convolution fusion | flops 254803968 | bytes 5833728 | tf_op jit(solution)/shard_map/transpose | solution.py:114
  79.9 0.6 slice.33
  80.5 231.1 %all-reduce.4.cloned.1.call-done = (f32[10368,384]{1,0:T(8,128)}, f32[3456,384]{1,0:T(8,128)}) async-done(((f32[10368,384]{1,0:T(8,128)}, f32[3456,384]{1,0:T(8,128)}), (f32[10368,384]{1,0:T(8,128)}, f32[3456,384]{1,0:T(8,128)})) %all-reduce.4.cloned.1.call-update) | async-done | bytes 21233680 | tf_op jit(solution)/shard_map/psum | solution.py:140
  311.6 0.9 constant_dynamic-slice_fusion.1
  312.6 0.7 reshape.166
  313.2 0.8 constant_dynamic-slice_fusion
  (97 shorter events, 6.6 us)
Async XLA Ops:
  7.2 21.4 %copy-start = (bf16[3456,384]{1,0:T(8,128)(2,1)S(1)}, bf16[3456,384]{1,0:T(8,128)(2,1)}, u32[]{:S(2)}) copy-start(bf16[3456,384]{1,0:T(8,128)(2,1)} %param.9) | copy-start | bytes 7962628
  7.2 21.1 %copy-start.16 = (bf16[2,2,1,24,384]{4,3,2,1,0:T(8,128)(2,1)S(1)}, bf16[2,2,1,24,384]{4,3,2,1,0:T(8,128)(2,1)}, u32[]{:S(2)}) copy-start(bf16[2,2,1,24,384]{4,3,2,1,0:T(8,128)(2,1)} %param.11) | copy-start | bytes 221188
  7.2 20.9 %copy-start.19 = (bf16[384]{0:T(512)(128)(2,1)S(1)}, bf16[384]{0:T(512)(128)(2,1)}, u32[]{:S(2)}) copy-start(bf16[384]{0:T(512)(128)(2,1)} %param.8) | copy-start | bytes 2308
  7.2 304.4 %all-reduce.4.cloned.1.call-start = ((), (), s32[]{:S(2)}) async-start(), calls=%async_computation | async-start | bytes 42467328 | tf_op jit(solution)/shard_map/psum | solution.py:140
  9.1 19.5 %copy-start.18 = (pred[32,8]{0,1:T(8,128)(4,1)S(1)}, pred[32,8]{0,1:T(8,128)(4,1)}, u32[]{:S(2)}) copy-start(pred[32,8]{0,1:T(8,128)(4,1)} %constant.61) | copy-start | bytes 772
  10.4 8.3 %copy-start.1 = (bf16[2,2,2,48,384]{4,0,3,2,1:T(2,128)(2,1)}, bf16[2,2,2,48,384]{4,0,3,2,1:T(2,128)(2,1)S(1)}, u32[]{:S(2)}) copy-start(bf16[2,2,2,48,384]{4,0,3,2,1:T(2,128)(2,1)S(1)} %copy_multiply_fusion) | copy-start | bytes 884740
  10.9 17.3 %collective-permute-start.3 = (bf16[288,384]{1,0:T(8,128)(2,1)S(1)}, bf16[288,384]{1,0:T(8,128)(2,1)S(1)}, u32[]{:S(2)}, u32[]{:S(2)}) collective-permute-start(bf16[288,384]{1,0:T(8,128)(2,1)S(1)} %bitcast.105), channel_id=1, source_target_pairs={{0,1},{1,2},{2,3},{3,4},{4,5},{5,6},{6,7},{7,8},{8,9},{9,10},{10,1... | collective-permute-start | bytes 663560 | tf_op jit(solution)/shard_map/ppermute | solution.py:28
  15.9 12.2 %collective-permute-start = (bf16[192,384]{1,0:T(8,128)(2,1)S(1)}, bf16[192,384]{1,0:T(8,128)(2,1)S(1)}, u32[]{:S(2)}, u32[]{:S(2)}) collective-permute-start(bf16[192,384]{1,0:T(8,128)(2,1)S(1)} %bitcast.108), channel_id=1, source_target_pairs={{0,17},{1,18},{2,19},{3,20},{4,21},{5,22},{6,23},{7,24},{8,25},{9,... | collective-permute-start | bytes 442376 | tf_op jit(solution)/shard_map/ppermute | solution.py:28
  19.5 11.8 %collective-permute-start.4 = (bf16[384,384]{1,0:T(8,128)(2,1)}, bf16[384,384]{1,0:T(8,128)(2,1)}, u32[]{:S(2)}, u32[]{:S(2)}) collective-permute-start(bf16[384,384]{1,0:T(8,128)(2,1)} %bitcast.2), channel_id=1, source_target_pairs={{1,0},{2,1},{3,2},{4,3},{5,4},{6,5},{7,6},{8,7},{9,8},{10,9},{11,1... | collective-permute-start | bytes 884744 | tf_op jit(solution)/shard_map/ppermute | solution.py:28
  22.0 11.1 %collective-permute-start.2 = (bf16[384,384]{1,0:T(8,128)(2,1)}, bf16[384,384]{1,0:T(8,128)(2,1)}, u32[]{:S(2)}, u32[]{:S(2)}) collective-permute-start(bf16[384,384]{1,0:T(8,128)(2,1)} %bitcast.2), channel_id=1, source_target_pairs={{1,16},{2,17},{3,18},{4,19},{5,20},{6,21},{7,22},{8,23},{9,24},{10... | collective-permute-start | bytes 884744 | tf_op jit(solution)/shard_map/ppermute | solution.py:28
  25.2 9.5 %collective-permute-start.1 = (bf16[384,384]{1,0:T(8,128)(2,1)}, bf16[384,384]{1,0:T(8,128)(2,1)}, u32[]{:S(2)}, u32[]{:S(2)}) collective-permute-start(bf16[384,384]{1,0:T(8,128)(2,1)} %bitcast.2), channel_id=1, source_target_pairs={{0,16},{16,32},{32,48},{48,64},{64,80},{80,96},{96,112},{1,17},{17... | collective-permute-start | bytes 884744 | tf_op jit(solution)/shard_map/ppermute | solution.py:28
  28.2 7.8 %copy-start.12 = (bf16[2,2,1,48,384]{4,0,3,2,1:T(2,128)(2,1)}, bf16[2,2,1,48,384]{4,0,3,2,1:T(2,128)(2,1)S(1)}, u32[]{:S(2)}) copy-start(bf16[2,2,1,48,384]{4,0,3,2,1:T(2,128)(2,1)S(1)} %copy.53) | copy-start | bytes 442372
  29.8 6.2 %copy-start.14 = (bf16[2,2,1,48,384]{4,0,3,2,1:T(2,128)(2,1)}, bf16[2,2,1,48,384]{4,0,3,2,1:T(2,128)(2,1)S(1)}, u32[]{:S(2)}) copy-start(bf16[2,2,1,48,384]{4,0,3,2,1:T(2,128)(2,1)S(1)} %copy.84) | copy-start | bytes 442372
  30.3 6.5 %copy-start.2 = (bf16[2,2,2,48,384]{4,0,3,2,1:T(2,128)(2,1)S(1)}, bf16[2,2,2,48,384]{4,0,3,2,1:T(2,128)(2,1)}, u32[]{:S(2)}) copy-start(bf16[2,2,2,48,384]{4,0,3,2,1:T(2,128)(2,1)} %copy-done.1) | copy-start | bytes 884740
  30.3 10.5 %slice-start = ((s8[7962624]{0:T(1024)(128)(4,1)}), s8[4194304]{0:T(1024)(128)(4,1)S(1)}, s32[]{:S(2)}) async-start(s8[7962624]{0:T(1024)(128)(4,1)} %bitcast.111), calls=%async_computation.1 | async-start | bytes 8388608
  33.1 2.9 copy-start.6
  34.5 1.5 copy-start.8
  36.0 0.7 copy-start.10
  39.0 2.1 slice-start.1
  40.3 0.8 copy-start.20
  58.7 1.8 copy-start.4
  60.3 1.2 copy-start.3
  60.3 1.2 copy-start.7
  60.3 1.2 copy-start.9
  60.3 1.2 copy-start.11
  60.3 1.2 copy-start.13
  60.3 1.3 copy-start.15
  61.6 13.5 %copy-start.5 = (bf16[4,3,49,384]{3,0,2,1:T(4,128)(2,1)S(1)}, bf16[4,3,49,384]{3,0,2,1:T(4,128)(2,1)}, u32[]{:S(2)}) copy-start(bf16[4,3,49,384]{3,0,2,1:T(4,128)(2,1)} %reshape.160) | copy-start | bytes 1354756
  61.6 13.5 %copy-start.17 = (bf16[2,2,1,24,384]{4,3,2,1,0:T(8,128)(2,1)S(1)}, bf16[2,2,1,24,384]{4,3,2,1,0:T(8,128)(2,1)}, u32[]{:S(2)}) copy-start(bf16[2,2,1,24,384]{4,3,2,1,0:T(8,128)(2,1)} %param.11) | copy-start | bytes 221188
  78.5 0.7 copy-start.21
Sparse Core Ops, SparseCore 0:
  78.6 232.9 all-reduce.3
